TPU v7x, 256 devices: a whole 4x4x8 slice. The times are simulated.
256 devices in a mesh: dp: 4 (over x), feat: 8 (over y, core), cent: 8 (over z).
Axes of the slice: x: 4, y: 4, z: 8, core: 2. Of those that a mesh axis runs over, the one named last changes fastest.
Arguments:
- embeddings: bfloat16 [8192, 768], P(('dp', 'cent')), may hold values from -12 to 12
- projection: bfloat16 [768, 8192], P(None, 'feat'), may hold values from -0.21875 to 0.21875
- phases: float32 [8192], P('feat'), may hold values from -4 to 4
- centroids: bfloat16 [4096, 8192], P('cent', 'feat'), may hold values from -7 to 7
Outputs:
- updated: float32 [4096, 8192], P('cent', 'feat')
All inputs are finite; a program needn't handle non-finite values.
Results may differ from a plain program's by a relative error of at most 0.0003.
Values may be sent and summed in bfloat16 or wider, within the bound.
No kernel may reach another device: no remote copies, remote signals or barrier semaphores. Data moves between devices by JAX's collectives and lax.ppermute only.
A program may use at most 64 MiB of HBM per device.

v0:
```python
import math

import jax
import jax.numpy as jnp
from jax import lax
from jax.sharding import PartitionSpec as P

F = 8192


SQRT_TWO = math.sqrt(2.0)
SHARP_FACTOR = 1.5
PRIOR_MASS = 1.0


def featurize(embeddings, projection, phases):
    projected = jnp.dot(embeddings, projection, preferred_element_type=jnp.float32)
    return (SQRT_TWO * jnp.cos(projected + phases)).astype(jnp.bfloat16)


def score_part(features, centers):
    center_wide = centers.astype(jnp.float32)
    center_sq = jnp.sum(center_wide * center_wide, axis=1)
    inner_part = lax.dot_general(
        features, centers, (((1,), (1,)), ((), ())), preferred_element_type=jnp.float32
    )
    return 2.0 * inner_part - center_sq[None, :]


def row_contract(weights, features):
    return lax.dot_general(
        weights, features, (((0,), (0,)), ((), ())), preferred_element_type=jnp.float32
    )


def local_softmax(logits):
    top_score = jnp.max(logits, axis=1, keepdims=True)
    exp_terms = jnp.exp(logits - top_score)
    return (exp_terms / jnp.sum(exp_terms, axis=1, keepdims=True)).astype(jnp.bfloat16)


def responsibilities(partial_value, sharpness, normalize):
    return normalize(sharpness * lax.psum(partial_value, "feat"))


def shards(embeddings, projection, phases, centroids):
    features = featurize(embeddings, projection, phases)
    sharpness = SHARP_FACTOR / math.sqrt(F)
    local_rows = features.shape[0]
    local_cent = centroids.shape[0]
    n_data = lax.axis_size("dp")
    n_groups = lax.axis_size("cent")
    partial_value = score_part(features, lax.all_gather(centroids, "cent", axis=0, tiled=True))
    resp = responsibilities(partial_value, sharpness, local_softmax)
    block_rows = local_cent // n_data
    total_cent = resp.shape[1]
    reordered = (
        resp.reshape(local_rows, n_groups, n_data, block_rows)
        .transpose(0, 2, 1, 3)
        .reshape(local_rows, total_cent)
    )
    sums_block, mass_block = lax.psum_scatter(
        (row_contract(reordered, features), jnp.sum(reordered.astype(jnp.float32), axis=0)),
        ("dp", "cent"),
        scatter_dimension=0,
        tiled=True,
    )
    old_block = lax.dynamic_slice_in_dim(
        centroids, lax.axis_index("dp") * block_rows, block_rows, 0
    ).astype(jnp.float32)
    fresh_block = (sums_block + PRIOR_MASS * old_block) / (mass_block + PRIOR_MASS)[:, None]
    updated = lax.all_gather(fresh_block, "dp", axis=0, tiled=True)
    return updated


def solution(mesh):
    return jax.shard_map(
        shards,
        mesh=mesh,
        in_specs=(P(("dp", "cent"), None), P(None, "feat"), P("feat"), P("cent", "feat")),
        out_specs=P("cent", "feat"),
        check_vma=False,
    )
```

profile of v0, /device:TPU:1, one launch (start us, length us, event | category | flops | bytes accessed | tf_op | source)
XLA Modules:
  0.0 508.9 jit_solution(3235812730124136146)
XLA Ops:
  6.5 0.0 copy-start
  6.5 0.0 all-gather.3.cloned.1.call-start
  6.5 0.7 all-gather.3.cloned.1.call-update
  7.3 0.0 all-reduce.3.cloned.1.call-start
  7.3 0.6 copy-done
  7.9 5.4 %fusion.4 = bf16[256,1024]{1,0:T(8,128)(2,1)S(1)} fusion(bf16[256,768]{1,0:T(8,128)(2,1)} %param.4, bf16[768,1024]{1,0:T(8,128)(2,1)S(1)} %copy-done, f32[1024]{0:T(1024)} %param.6), kind=kOutput, calls=%fused_computation.11 | convolution fusion | flops 403439616 | bytes 2494464 | tf_op jit(solution)/shard_map/dot_general | solution.py:17
  13.3 93.5 %all-gather.3.cloned.1.call-done = bf16[4096,1024]{1,0:T(8,128)(2,1)} async-done(((bf16[512,1024]{1,0:T(8,128)(2,1)}), bf16[4096,1024]{1,0:T(8,128)(2,1)}) %all-gather.3.cloned.1.call-update) | async-done | bytes 8388624 | tf_op jit(solution)/shard_map/all_gather | solution.py:53
  106.9 5.2 %multiply_reduce_fusion = f32[4096]{0:T(1024)S(1)} fusion(bf16[4096,1024]{1,0:T(8,128)(2,1)} %all-gather.3.cloned.1.call-done), kind=kLoop, calls=%fused_computation | loop fusion | flops 12578816 | bytes 8404992 | tf_op jit(solution)/shard_map/reduce_sum | solution.py:23
  112.1 0.5 copy-done.2
  112.6 4.4 fusion
  117.0 0.0 all-reduce.3.cloned.1.call-update
  117.0 0.0 reduce-scatter.2.cloned.1.call-start
  117.1 74.7 %all-reduce.3.cloned.1.call-done = f32[256,4096]{1,0:T(8,128)} async-done(((f32[256,4096]{1,0:T(8,128)}), f32[256,4096]{1,0:T(8,128)}) %all-reduce.3.cloned.1.call-update) | async-done | bytes 4194320 | tf_op jit(solution)/shard_map/psum | solution.py:43
  191.8 2.7 multiply_reduce_fusion.1
  194.5 0.7 copy-done.1
  195.2 0.8 fusion.1
  196.1 2.3 divide_convert_fusion
  198.3 4.4 reshape.12
  202.8 4.3 copy.6
  207.0 9.7 %fusion.5 = f32[4096,1024]{1,0:T(8,128)} fusion(bf16[256,4096]{0,1:T(8,128)(2,1)} %bitcast.12, bf16[256,1024]{1,0:T(8,128)(2,1)S(1)} %fusion.4), kind=kOutput, calls=%fused_computation.14 | convolution fusion | flops 2147483648 | bytes 19398656 | tf_op jit(solution)/shard_map/dot_general | solution.py:31
  216.7 0.0 reduce-scatter.2.cloned.1.call-update
  216.7 0.0 all-gather.5.cloned.1.call-start
  216.8 0.6 copy-done.3
  217.4 0.6 dynamic-slice
  218.5 2.2 convert_reduce_fusion
  220.7 116.8 %all-reduce = f32[4096]{0:T(1024)S(1)} all-reduce(f32[4096]{0:T(1024)S(1)} %bitcast.13), channel_id=3, replica_groups=mesh['dp'=4,'feat'=8,'cent'=8] {'dp','cent'}, use_global_device_ids=true, to_apply=%region_6.0.clone | all-reduce | flops 4096 | bytes 32768
  337.5 0.1 dynamic-slice_add_fusion
  337.6 123.6 %reduce-scatter.2.cloned.1.call-done = f32[128,1024]{1,0:T(8,128)} async-done(((f32[4096,1024]{1,0:T(8,128)}), f32[128,1024]{1,0:T(8,128)}) %reduce-scatter.2.cloned.1.call-update) | async-done | bytes 524304 | tf_op jit(solution)/shard_map/reduce_scatter | solution.py:62
  461.2 2.0 add_divide_fusion
  463.2 0.0 all-gather.5.cloned.1.call-update
  463.2 36.0 %all-gather.5.cloned.1.call-done = f32[512,1024]{1,0:T(8,128)} async-done(((f32[128,1024]{1,0:T(8,128)}), f32[512,1024]{1,0:T(8,128)}) %all-gather.5.cloned.1.call-update) | async-done | bytes 2097168 | tf_op jit(solution)/shard_map/all_gather | solution.py:72
  499.2 3.2 copy.9
  (3 shorter events, 0.0 us)
Async XLA Ops:
  6.5 1.4 copy-start
  6.5 100.3 %all-gather.3.cloned.1.call-start = ((), (), s32[]{:S(2)}) async-start(), calls=%async_computation.1 | async-start | bytes 9437184 | tf_op jit(solution)/shard_map/all_gather | solution.py:53
  7.3 184.5 %all-reduce.3.cloned.1.call-start = ((), (), s32[]{:S(2)}) async-start(), calls=%async_computation.2 | async-start | bytes 8388608 | tf_op jit(solution)/shard_map/psum | solution.py:43
  106.9 5.8 %copy-start.2 = (bf16[4096,1024]{1,0:T(8,128)(2,1)S(1)}, bf16[4096,1024]{1,0:T(8,128)(2,1)}, u32[]{:S(2)}) copy-start(bf16[4096,1024]{1,0:T(8,128)(2,1)} %all-gather.3.cloned.1.call-done) | copy-start | bytes 25165828
  117.0 344.2 %reduce-scatter.2.cloned.1.call-start = ((), (), s32[]{:S(2)}) async-start(), calls=%async_computation.3 | async-start | bytes 17301504 | tf_op jit(solution)/shard_map/reduce_scatter | solution.py:62
  191.8 3.4 copy-start.1
  216.7 0.7 copy-start.3
  216.7 282.5 %all-gather.5.cloned.1.call-start = ((), (), s32[]{:S(2)}) async-start(), calls=%async_computation.4 | async-start | bytes 2621440 | tf_op jit(solution)/shard_map/all_gather | solution.py:72
Sparse Core Ops, SparseCore 0:
  9.1 97.6 all-gather.2
  117.1 74.5 all-reduce.2
  216.8 244.2 reduce-scatter.1
  463.3 35.7 all-gather.4
where the time goes:
time: 509 us
  waiting for transfers between devices  329 us (65%)
  blocking collectives  117 us (23%)
  matrix products  19.4 us (4%)
  other arithmetic  15.4 us (3%)
  local copies, waits for them, and re-layouts  14.9 us (3%)
  between operations  13.7 us (3%)
    reduce_scatter x1, waiting for transfers between devices, shards(): lax.psum_scatter((row_contract(reordered, features), jnp.sum(reordered.as...  124 us
    unnamed x1, blocking collectives  117 us
    all_gather x1, waiting for transfers between devices, shards(): lax.all_gather(centroids, 'cent', axis=0, tiled=True)  93.5 us
    psum x1, waiting for transfers between devices, responsibilities(): return normalize(sharpness * lax.psum(partial_value, 'feat'))  74.7 us
    all_gather x1, waiting for transfers between devices, shards(): updated = lax.all_gather(fresh_block, 'dp', axis=0, tiled=True)  36 us
  transfers between devices with their start and end apart: 4, of which 4 were waited for; matrix products, arithmetic and copies ran while one was open for 2% of the time, Pallas kernels for 0%

commit v1 on v0

v1 whole, which is shorter than its diff:
```python
import math

import jax
import jax.numpy as jnp
from jax import lax
from jax.sharding import PartitionSpec as P

F = 8192


SQRT_TWO = math.sqrt(2.0)
SHARP_FACTOR = 1.5
PRIOR_MASS = 1.0


def featurize(embeddings, projection, phases):
    projected = jnp.dot(embeddings, projection, preferred_element_type=jnp.float32)
    return (SQRT_TWO * jnp.cos(projected + phases)).astype(jnp.bfloat16)


def shards(embeddings, projection, phases, centroids):
    features = featurize(embeddings, projection, phases)
    group_features = lax.all_gather(features, "cent", axis=0, tiled=True)
    sharpness = SHARP_FACTOR / math.sqrt(F)

    center_wide = centroids.astype(jnp.float32)
    center_sq = jnp.sum(center_wide * center_wide, axis=1)
    inner_part = lax.dot_general(
        group_features, centroids, (((1,), (1,)), ((), ())), preferred_element_type=jnp.float32
    )
    partial_value = 2.0 * inner_part - center_sq[None, :]
    logits = sharpness * lax.psum_scatter(partial_value, "feat", scatter_dimension=0, tiled=True)

    local_top = jnp.max(logits, axis=1)
    local_sum = jnp.sum(jnp.exp(logits - local_top[:, None]), axis=1)
    stats = lax.all_gather(jnp.stack([local_top, local_sum]), "cent", axis=0)
    top_score = jnp.max(stats[:, 0], axis=0)
    total = jnp.sum(stats[:, 1] * jnp.exp(stats[:, 0] - top_score[None, :]), axis=0)
    resp = (jnp.exp(logits - top_score[:, None]) / total[:, None]).astype(jnp.bfloat16)

    group_resp = lax.all_gather(resp, "feat", axis=0, tiled=True)
    mass_part = jnp.sum(group_resp.astype(jnp.float32), axis=0)
    sums_part = lax.dot_general(
        group_resp, group_features, (((0,), (0,)), ((), ())), preferred_element_type=jnp.float32
    )
    width = sums_part.shape[1]
    mass_rows = -(-mass_part.shape[0] // width)
    mass_block = jnp.pad(mass_part, (0, mass_rows * width - mass_part.shape[0])).reshape(mass_rows, width)
    both = lax.psum(jnp.concatenate([sums_part, mass_block], axis=0), "dp")
    sums = both[: sums_part.shape[0]]
    mass = both[sums_part.shape[0] :].reshape(-1)[: mass_part.shape[0]]
    return (sums + PRIOR_MASS * center_wide) / (mass + PRIOR_MASS)[:, None]


def solution(mesh):
    return jax.shard_map(
        shards,
        mesh=mesh,
        in_specs=(P(("dp", "cent"), None), P(None, "feat"), P("feat"), P("cent", "feat")),
        out_specs=P("cent", "feat"),
        check_vma=False,
    )
```

time: 509 us -> 255 us (0.50)
  waiting for transfers between devices: 329 us -> 192 us
  blocking collectives: 117 us -> 18.2 us
  local copies, waits for them, and re-layouts: 14.9 us -> 1.41 us
    unnamed x1 -> x0, blocking collectives: 117 us -> none
    reduce_scatter x1, waiting for transfers between devices: 124 us -> 36.6 us  [shards(): lax.psum_scatter(partial_value, 'feat', scatter_dimension=0, tiled=True)]
    all_gather x2, waiting for transfers between devices: 129 us -> 91 us  [the longest x1 58.2 us: shards(): group_features = lax.all_gather(features, 'cent', axis=0, tiled=True)]
    all_gather x0 -> x1, blocking collectives: none -> 18.2 us  [shards(): stats = lax.all_gather(jnp.stack([local_top, local_sum]), 'cent', axis=0)]
    psum x1, waiting for transfers between devices: 74.7 us -> 64.3 us  [shards(): both = lax.psum(jnp.concatenate([sums_part, mass_block], axis=0), 'dp')]
    reshape x2 -> x0, local copies, waits for them, and re-layouts: 8.7 us -> none  [shards(): resp.reshape(local_rows, n_groups, n_data, block_rows).transpose(0, 2, 1, 3)]
  transfers between devices with their start and end apart: 4 -> 4, of which waited for: 4 -> 4; matrix products, arithmetic and copies ran while one was open for 2% -> 0% of each run, Pallas kernels for 0% -> 0%
where the time goes in v1:
time: 255 us
  waiting for transfers between devices  192 us (75%)
  blocking collectives  18.2 us (7%)
  matrix products  17.5 us (7%)
  between operations  13.2 us (5%)
  other arithmetic  12.3 us (5%)
    psum x1, waiting for transfers between devices, shards(): both = lax.psum(jnp.concatenate([sums_part, mass_block], axis=0), 'dp')  64.3 us
    all_gather x1, waiting for transfers between devices, shards(): group_features = lax.all_gather(features, 'cent', axis=0, tiled=True)  58.2 us
    reduce_scatter x1, waiting for transfers between devices, shards(): lax.psum_scatter(partial_value, 'feat', scatter_dimension=0, tiled=True)  36.6 us
    all_gather x1, waiting for transfers between devices, shards(): group_resp = lax.all_gather(resp, 'feat', axis=0, tiled=True)  32.8 us
    all_gather x1, blocking collectives, shards(): stats = lax.all_gather(jnp.stack([local_top, local_sum]), 'cent', axis=0)  18.2 us
    dot_general x1, matrix products, shards(): lax.dot_general(group_features, centroids, (((1,), (1,)), ((), ())), pref...  6.54 us
    dot_general x1, matrix products, featurize(): jnp.dot(embeddings, projection, preferred_element_type=jnp.float32)  5.75 us
    dot_general x1, matrix products, shards(): lax.dot_general(group_resp, group_features, (((0,), (0,)), ((), ())), pre...  5.16 us
  transfers between devices with their start and end apart: 4, of which 4 were waited for; matrix products, arithmetic and copies ran while one was open for 0% of the time, Pallas kernels for 0%

profile of v1, /device:TPU:1, one launch (start us, length us, event | category | flops | bytes accessed | tf_op | source)
XLA Modules:
  0.0 254.6 jit_solution(12030639300584852674)
XLA Ops:
  6.5 0.0 copy-start
  6.5 0.0 copy-start.1
  6.5 0.0 all-gather.5.cloned.1.call-start
  6.5 1.4 copy-done
  7.9 5.8 %fusion.4 = bf16[256,1024]{1,0:T(8,128)(2,1)} fusion(bf16[256,768]{1,0:T(8,128)(2,1)} %param.4, bf16[768,1024]{1,0:T(8,128)(2,1)S(1)} %copy-done, f32[1024]{0:T(1024)} %param.6), kind=kOutput, calls=%fused_computation.10 | convolution fusion | flops 403439616 | bytes 2494464 | tf_op jit(solution)/shard_map/dot_general | solution.py:17
  13.7 0.0 all-gather.5.cloned.1.call-update
  13.7 0.0 reduce-scatter.2.cloned.1.call-start
  13.8 0.0 copy-done.1
  13.8 0.3 fusion
  14.1 58.2 %all-gather.5.cloned.1.call-done = bf16[2048,1024]{1,0:T(8,128)(2,1)} async-done(((bf16[256,1024]{1,0:T(8,128)(2,1)}), bf16[2048,1024]{1,0:T(8,128)(2,1)}) %all-gather.5.cloned.1.call-update) | async-done | bytes 4194320 | tf_op jit(solution)/shard_map/all_gather | solution.py:23
  72.3 6.5 %multiply_subtract_fusion = f32[2048,512]{1,0:T(8,128)} fusion(bf16[2048,1024]{1,0:T(8,128)(2,1)} %all-gather.5.cloned.1.call-done, bf16[512,1024]{1,0:T(8,128)(2,1)S(1)} %copy-done.1, f32[512]{0:T(512)S(1)} %fusion), kind=kOutput, calls=%fused_computation.1 | convolution fusion | flops 2149580800 | bytes 9439232 | tf_op jit(solution)/shard_map/dot_general | solution.py:28
  78.8 0.0 reduce-scatter.2.cloned.1.call-update
  78.8 0.0 all-gather.7.cloned.1.call-start
  78.9 36.6 %reduce-scatter.2.cloned.1.call-done = f32[256,512]{1,0:T(8,128)} async-done(((f32[2048,512]{1,0:T(8,128)}), f32[256,512]{1,0:T(8,128)}) %reduce-scatter.2.cloned.1.call-update) | async-done | bytes 524304 | tf_op jit(solution)/shard_map/reduce_scatter | solution.py:32
  115.5 1.2 multiply_reduce_fusion
  116.7 1.3 exponential_reduce_fusion
  117.9 18.2 %all-gather.1 = f32[8,2,256]{2,1,0:T(2,128)S(1)} all-gather(f32[1,2,256]{2,1,0:T(2,128)S(1)} %maximum_bitcast_fusion), channel_id=2, replica_groups=mesh['dp'=4,'feat'=8,'cent'=8] {'cent'}, dimensions={0}, use_global_device_ids=true | all-gather | bytes 18432 | tf_op jit(solution)/shard_map/all_gather | solution.py:36
  136.2 1.9 divide_convert_fusion
  138.2 0.0 all-gather.7.cloned.1.call-update
  138.2 0.0 all-reduce.3.cloned.1.call-start
  138.2 32.8 %all-gather.7.cloned.1.call-done = bf16[2048,512]{1,0:T(8,128)(2,1)} async-done(((bf16[256,512]{1,0:T(8,128)(2,1)}), bf16[2048,512]{1,0:T(8,128)(2,1)}) %all-gather.7.cloned.1.call-update) | async-done | bytes 2097168 | tf_op jit(solution)/shard_map/all_gather | solution.py:41
  171.0 1.9 convert_reduce_fusion
  173.0 5.2 %fusion.8 = f32[512,1024]{1,0:T(8,128)S(1)} fusion(bf16[2048,512]{1,0:T(8,128)(2,1)} %all-gather.7.cloned.1.call-done, bf16[2048,1024]{1,0:T(8,128)(2,1)} %all-gather.5.cloned.1.call-done), kind=kOutput, calls=%fused_computation.22 | convolution fusion | flops 2147483648 | bytes 8388608 | tf_op jit(solution)/shard_map/dot_general | solution.py:43
  178.1 1.6 pad_maximum_fusion
  179.7 0.0 all-reduce.3.cloned.1.call-update
  179.8 64.3 %all-reduce.3.cloned.1.call-done = f32[513,1024]{1,0:T(8,128)} async-done(((f32[513,1024]{1,0:T(8,128)}), f32[513,1024]{1,0:T(8,128)}) %all-reduce.3.cloned.1.call-update) | async-done | bytes 2101264 | tf_op jit(solution)/shard_map/psum | solution.py:49
  244.0 0.7 slice_add_fusion
  244.8 3.3 %fusion.1 = f32[512,1024]{1,0:T(8,128)} fusion(bf16[512,1024]{1,0:T(8,128)(2,1)S(1)} %copy-done.1, f32[513,1024]{1,0:T(8,128)} %all-reduce.3.cloned.1.call-done, f32[512]{0:T(512)S(1)} %bitcast.26), kind=kLoop, calls=%fused_computation.6 | loop fusion | flops 1572864 | bytes 5244928 | tf_op jit(solution)/shard_map/div | solution.py:52
  (4 shorter events, 0.1 us)
Async XLA Ops:
  6.5 1.4 copy-start
  6.5 7.2 %copy-start.1 = (bf16[512,1024]{1,0:T(8,128)(2,1)S(1)}, bf16[512,1024]{1,0:T(8,128)(2,1)}, u32[]{:S(2)}) copy-start(bf16[512,1024]{1,0:T(8,128)(2,1)} %param.7) | copy-start | bytes 3145732
  6.5 65.7 %all-gather.5.cloned.1.call-start = ((), (), s32[]{:S(2)}) async-start(), calls=%async_computation.1 | async-start | bytes 4718592 | tf_op jit(solution)/shard_map/all_gather | solution.py:23
  13.7 101.8 %reduce-scatter.2.cloned.1.call-start = ((), (), s32[]{:S(2)}) async-start(), calls=%async_computation.2 | async-start | bytes 4718592 | tf_op jit(solution)/shard_map/reduce_scatter | solution.py:32
  78.8 92.2 %all-gather.7.cloned.1.call-start = ((), (), s32[]{:S(2)}) async-start(), calls=%async_computation.3 | async-start | bytes 2359296 | tf_op jit(solution)/shard_map/all_gather | solution.py:41
  138.2 105.9 %all-reduce.3.cloned.1.call-start = ((), (), s32[]{:S(2)}) async-start(), calls=%async_computation.4 | async-start | bytes 4259840 | tf_op jit(solution)/shard_map/psum | solution.py:49
Sparse Core Ops, SparseCore 0:
  13.8 58.3 all-gather.4
  78.9 36.5 reduce-scatter.1
  138.3 32.6 all-gather.6
  179.9 64.1 all-reduce.2

commit v2 on v1

--- a/solution.py
+++ b/solution.py
@@ -33,7 +33,12 @@
 
     local_top = jnp.max(logits, axis=1)
     local_sum = jnp.sum(jnp.exp(logits - local_top[:, None]), axis=1)
-    stats = lax.all_gather(jnp.stack([local_top, local_sum]), "cent", axis=0)
+    pair = jnp.stack([local_top, local_sum])
+    n_cent = lax.axis_size("cent")
+    received = [pair]
+    for shift in range(1, n_cent):
+        received.append(lax.ppermute(pair, "cent", [(i, (i + shift) % n_cent) for i in range(n_cent)]))
+    stats = jnp.stack(received)
     top_score = jnp.max(stats[:, 0], axis=0)
     total = jnp.sum(stats[:, 1] * jnp.exp(stats[:, 0] - top_score[None, :]), axis=0)
     resp = (jnp.exp(logits - top_score[:, None]) / total[:, None]).astype(jnp.bfloat16)

time: 255 us -> 250 us (0.980)
  blocking collectives: 18.2 us -> 0 us
  starting transfers between devices: 0.13 us -> 15.2 us
    all_gather x1 -> x0, blocking collectives: 18.2 us -> none  [shards(): stats = lax.all_gather(jnp.stack([local_top, local_sum]), 'cent', axis=0)]
    ppermute x0 -> x7, starting transfers between devices: none -> 14.9 us  [shards(): lax.ppermute(pair, 'cent', [(i, (i + shift) % n_cent) for i in range(n_ce...]
    all_gather x1, waiting for transfers between devices: 32.8 us -> 29.7 us  [shards(): group_resp = lax.all_gather(resp, 'feat', axis=0, tiled=True)]
  transfers between devices with their start and end apart: 4 -> 11, of which waited for: 4 -> 5; matrix products, arithmetic and copies ran while one was open for 0% -> 0% of each run, Pallas kernels for 0% -> 0%
where the time goes in v2:
time: 250 us
  waiting for transfers between devices  190 us (76%)
  matrix products  17.5 us (7%)
  starting transfers between devices  15.2 us (6%)
  between operations  13.2 us (5%)
  other arithmetic  12.2 us (5%)
    psum x1, waiting for transfers between devices, shards(): both = lax.psum(jnp.concatenate([sums_part, mass_block], axis=0), 'dp')  64.3 us
    all_gather x1, waiting for transfers between devices, shards(): group_features = lax.all_gather(features, 'cent', axis=0, tiled=True)  58.2 us
    reduce_scatter x1, waiting for transfers between devices, shards(): lax.psum_scatter(partial_value, 'feat', scatter_dimension=0, tiled=True)  36.6 us
    all_gather x1, waiting for transfers between devices, shards(): group_resp = lax.all_gather(resp, 'feat', axis=0, tiled=True)  29.7 us
    ppermute x7, starting transfers between devices, shards(): lax.ppermute(pair, 'cent', [(i, (i + shift) % n_cent) for i in range(n_ce...  14.9 us
    dot_general x1, matrix products, shards(): lax.dot_general(group_features, centroids, (((1,), (1,)), ((), ())), pref...  6.55 us
    dot_general x1, matrix products, featurize(): jnp.dot(embeddings, projection, preferred_element_type=jnp.float32)  5.76 us
    dot_general x1, matrix products, shards(): lax.dot_general(group_resp, group_features, (((0,), (0,)), ((), ())), pre...  5.16 us
  transfers between devices with their start and end apart: 11, of which 5 were waited for; matrix products, arithmetic and copies ran while one was open for 0% of the time, Pallas kernels for 0%

profile of v2, /device:TPU:1, one launch (start us, length us, event | category | flops | bytes accessed | tf_op | source)
XLA Modules:
  0.0 249.7 jit_solution(5364999765038315897)
XLA Ops:
  6.5 1.4 copy-done
  7.9 5.8 %fusion.4 = bf16[256,1024]{1,0:T(8,128)(2,1)} fusion(bf16[256,768]{1,0:T(8,128)(2,1)} %param.4, bf16[768,1024]{1,0:T(8,128)(2,1)S(1)} %copy-done, f32[1024]{0:T(1024)} %param.6), kind=kOutput, calls=%fused_computation.10 | convolution fusion | flops 403439616 | bytes 2494464 | tf_op jit(solution)/shard_map/dot_general | solution.py:17
  13.7 0.0 all-gather.3.cloned.1.call-update
  13.7 0.0 reduce-scatter.2.cloned.1.call-start
  13.8 0.3 fusion
  14.1 58.2 %all-gather.3.cloned.1.call-done = bf16[2048,1024]{1,0:T(8,128)(2,1)} async-done(((bf16[256,1024]{1,0:T(8,128)(2,1)}), bf16[2048,1024]{1,0:T(8,128)(2,1)}) %all-gather.3.cloned.1.call-update) | async-done | bytes 4194320 | tf_op jit(solution)/shard_map/all_gather | solution.py:23
  72.3 6.5 %multiply_subtract_fusion = f32[2048,512]{1,0:T(8,128)} fusion(bf16[2048,1024]{1,0:T(8,128)(2,1)} %all-gather.3.cloned.1.call-done, bf16[512,1024]{1,0:T(8,128)(2,1)S(1)} %copy-done.1, f32[512]{0:T(512)S(1)} %fusion), kind=kOutput, calls=%fused_computation.1 | convolution fusion | flops 2149580800 | bytes 9439232 | tf_op jit(solution)/shard_map/dot_general | solution.py:28
  78.8 0.0 reduce-scatter.2.cloned.1.call-update
  78.8 0.0 all-gather.5.cloned.1.call-start
  78.9 36.6 %reduce-scatter.2.cloned.1.call-done = f32[256,512]{1,0:T(8,128)} async-done(((f32[2048,512]{1,0:T(8,128)}), f32[256,512]{1,0:T(8,128)}) %reduce-scatter.2.cloned.1.call-update) | async-done | bytes 524304 | tf_op jit(solution)/shard_map/reduce_scatter | solution.py:32
  115.5 1.2 multiply_reduce_fusion
  116.7 1.3 exponential_reduce_fusion
  118.0 3.8 %collective-permute-start.5 = (f32[2,256]{1,0:T(2,128)S(1)}, f32[2,256]{1,0:T(2,128)S(1)}, u32[]{:S(2)}, u32[]{:S(2)}) collective-permute-start(f32[2,256]{1,0:T(2,128)S(1)} %get-tuple-element.5), channel_id=1, source_target_pairs={{0,6},{1,7},{2,0},{3,1},{4,2},{5,3},{6,4},{7,5},{8,14},{9,15},{10,... | collective-permute-start | bytes 6152 | tf_op jit(solution)/shard_map/ppermute | solution.py:40
  121.7 1.8 collective-permute-start.4
  123.5 2.8 %collective-permute-start.3 = (f32[2,256]{1,0:T(2,128)S(1)}, f32[2,256]{1,0:T(2,128)S(1)}, u32[]{:S(2)}, u32[]{:S(2)}) collective-permute-start(f32[2,256]{1,0:T(2,128)S(1)} %get-tuple-element.5), channel_id=1, source_target_pairs={{0,4},{1,5},{2,6},{3,7},{4,0},{5,1},{6,2},{7,3},{8,12},{9,13},{10,... | collective-permute-start | bytes 6152 | tf_op jit(solution)/shard_map/ppermute | solution.py:40
  126.3 0.4 collective-permute-start.2
  126.7 3.5 %collective-permute-start.1 = (f32[2,256]{1,0:T(2,128)S(1)}, f32[2,256]{1,0:T(2,128)S(1)}, u32[]{:S(2)}, u32[]{:S(2)}) collective-permute-start(f32[2,256]{1,0:T(2,128)S(1)} %get-tuple-element.5), channel_id=1, source_target_pairs={{0,2},{1,3},{2,4},{3,5},{4,6},{5,7},{6,0},{7,1},{8,10},{9,11},{10,... | collective-permute-start | bytes 6152 | tf_op jit(solution)/shard_map/ppermute | solution.py:40
  130.2 0.0 collective-permute-done.5
  130.2 0.4 collective-permute-start
  130.6 2.3 collective-permute-start.6
  133.0 1.2 collective-permute-done
  134.3 1.9 divide_convert_fusion
  136.2 0.0 all-gather.5.cloned.1.call-update
  136.2 0.2 all-reduce.3.cloned.1.call-start
  136.4 29.7 %all-gather.5.cloned.1.call-done = bf16[2048,512]{1,0:T(8,128)(2,1)} async-done(((bf16[256,512]{1,0:T(8,128)(2,1)}), bf16[2048,512]{1,0:T(8,128)(2,1)}) %all-gather.5.cloned.1.call-update) | async-done | bytes 2097168 | tf_op jit(solution)/shard_map/all_gather | solution.py:46
  166.1 1.9 convert_reduce_fusion
  168.1 5.2 %fusion.9 = f32[512,1024]{1,0:T(8,128)S(1)} fusion(bf16[2048,512]{1,0:T(8,128)(2,1)} %all-gather.5.cloned.1.call-done, bf16[2048,1024]{1,0:T(8,128)(2,1)} %all-gather.3.cloned.1.call-done), kind=kOutput, calls=%fused_computation.23 | convolution fusion | flops 2147483648 | bytes 8388608 | tf_op jit(solution)/shard_map/dot_general | solution.py:48
  173.2 1.6 pad_maximum_fusion
  174.8 0.0 all-reduce.3.cloned.1.call-update
  174.8 64.3 %all-reduce.3.cloned.1.call-done = f32[513,1024]{1,0:T(8,128)} async-done(((f32[513,1024]{1,0:T(8,128)}), f32[513,1024]{1,0:T(8,128)}) %all-reduce.3.cloned.1.call-update) | async-done | bytes 2101264 | tf_op jit(solution)/shard_map/psum | solution.py:54
  239.1 0.7 slice_add_fusion
  239.8 3.3 %fusion.1 = f32[512,1024]{1,0:T(8,128)} fusion(bf16[512,1024]{1,0:T(8,128)(2,1)S(1)} %copy-done.1, f32[513,1024]{1,0:T(8,128)} %all-reduce.3.cloned.1.call-done, f32[512]{0:T(512)S(1)} %bitcast.32), kind=kLoop, calls=%fused_computation.6 | loop fusion | flops 1572864 | bytes 5244928 | tf_op jit(solution)/shard_map/div | solution.py:57
  (22 shorter events, 0.1 us)
Async XLA Ops:
  6.5 1.4 copy-start
  6.5 7.2 %copy-start.1 = (bf16[512,1024]{1,0:T(8,128)(2,1)S(1)}, bf16[512,1024]{1,0:T(8,128)(2,1)}, u32[]{:S(2)}) copy-start(bf16[512,1024]{1,0:T(8,128)(2,1)} %param.7) | copy-start | bytes 3145732
  6.5 65.7 %all-gather.3.cloned.1.call-start = ((), (), s32[]{:S(2)}) async-start(), calls=%async_computation.1 | async-start | bytes 4718592 | tf_op jit(solution)/shard_map/all_gather | solution.py:23
  13.7 101.8 %reduce-scatter.2.cloned.1.call-start = ((), (), s32[]{:S(2)}) async-start(), calls=%async_computation.2 | async-start | bytes 4718592 | tf_op jit(solution)/shard_map/reduce_scatter | solution.py:32
  78.8 87.3 %all-gather.5.cloned.1.call-start = ((), (), s32[]{:S(2)}) async-start(), calls=%async_computation.3 | async-start | bytes 2359296 | tf_op jit(solution)/shard_map/all_gather | solution.py:46
  118.0 12.3 %collective-permute-start.5 = (f32[2,256]{1,0:T(2,128)S(1)}, f32[2,256]{1,0:T(2,128)S(1)}, u32[]{:S(2)}, u32[]{:S(2)}) collective-permute-start(f32[2,256]{1,0:T(2,128)S(1)} %get-tuple-element.5), channel_id=1, source_target_pairs={{0,6},{1,7},{2,0},{3,1},{4,2},{5,3},{6,4},{7,5},{8,14},{9,15},{10,... | collective-permute-start | bytes 6152 | tf_op jit(solution)/shard_map/ppermute | solution.py:40
  121.7 8.8 %collective-permute-start.4 = (f32[2,256]{1,0:T(2,128)S(1)}, f32[2,256]{1,0:T(2,128)S(1)}, u32[]{:S(2)}, u32[]{:S(2)}) collective-permute-start(f32[2,256]{1,0:T(2,128)S(1)} %get-tuple-element.5), channel_id=1, source_target_pairs={{0,5},{1,6},{2,7},{3,0},{4,1},{5,2},{6,3},{7,4},{8,13},{9,14},{10,... | collective-permute-start | bytes 6152 | tf_op jit(solution)/shard_map/ppermute | solution.py:40
  123.5 9.4 %collective-permute-start.3 = (f32[2,256]{1,0:T(2,128)S(1)}, f32[2,256]{1,0:T(2,128)S(1)}, u32[]{:S(2)}, u32[]{:S(2)}) collective-permute-start(f32[2,256]{1,0:T(2,128)S(1)} %get-tuple-element.5), channel_id=1, source_target_pairs={{0,4},{1,5},{2,6},{3,7},{4,0},{5,1},{6,2},{7,3},{8,12},{9,13},{10,... | collective-permute-start | bytes 6152 | tf_op jit(solution)/shard_map/ppermute | solution.py:40
  126.3 6.6 %collective-permute-start.2 = (f32[2,256]{1,0:T(2,128)S(1)}, f32[2,256]{1,0:T(2,128)S(1)}, u32[]{:S(2)}, u32[]{:S(2)}) collective-permute-start(f32[2,256]{1,0:T(2,128)S(1)} %get-tuple-element.5), channel_id=1, source_target_pairs={{0,3},{1,4},{2,5},{3,6},{4,7},{5,0},{6,1},{7,2},{8,11},{9,12},{10,... | collective-permute-start | bytes 6152 | tf_op jit(solution)/shard_map/ppermute | solution.py:40
  126.7 6.2 %collective-permute-start.1 = (f32[2,256]{1,0:T(2,128)S(1)}, f32[2,256]{1,0:T(2,128)S(1)}, u32[]{:S(2)}, u32[]{:S(2)}) collective-permute-start(f32[2,256]{1,0:T(2,128)S(1)} %get-tuple-element.5), channel_id=1, source_target_pairs={{0,2},{1,3},{2,4},{3,5},{4,6},{5,7},{6,0},{7,1},{8,10},{9,11},{10,... | collective-permute-start | bytes 6152 | tf_op jit(solution)/shard_map/ppermute | solution.py:40
  130.2 3.9 %collective-permute-start = (f32[2,256]{1,0:T(2,128)S(1)}, f32[2,256]{1,0:T(2,128)S(1)}, u32[]{:S(2)}, u32[]{:S(2)}) collective-permute-start(f32[2,256]{1,0:T(2,128)S(1)} %get-tuple-element.5), channel_id=1, source_target_pairs={{0,1},{1,2},{2,3},{3,4},{4,5},{5,6},{6,7},{7,0},{8,9},{9,10},{10,1... | collective-permute-start | bytes 6152 | tf_op jit(solution)/shard_map/ppermute | solution.py:40
  130.6 3.6 %collective-permute-start.6 = (f32[2,256]{1,0:T(2,128)S(1)}, f32[2,256]{1,0:T(2,128)S(1)}, u32[]{:S(2)}, u32[]{:S(2)}) collective-permute-start(f32[2,256]{1,0:T(2,128)S(1)} %get-tuple-element.5), channel_id=1, source_target_pairs={{0,7},{1,0},{2,1},{3,2},{4,3},{5,4},{6,5},{7,6},{8,15},{9,8},{10,9... | collective-permute-start | bytes 6152 | tf_op jit(solution)/shard_map/ppermute | solution.py:40
  136.2 102.9 %all-reduce.3.cloned.1.call-start = ((), (), s32[]{:S(2)}) async-start(), calls=%async_computation.4 | async-start | bytes 4259840 | tf_op jit(solution)/shard_map/psum | solution.py:54
Sparse Core Ops, SparseCore 0:
  13.8 58.3 all-gather.2
  79.0 36.5 reduce-scatter.1
  136.3 29.7 all-gather.4
  175.0 64.1 all-reduce.2

commit v3 on v2

--- a/solution.py
+++ b/solution.py
@@ -29,7 +29,8 @@
         group_features, centroids, (((1,), (1,)), ((), ())), preferred_element_type=jnp.float32
     )
     partial_value = 2.0 * inner_part - center_sq[None, :]
-    logits = sharpness * lax.psum_scatter(partial_value, "feat", scatter_dimension=0, tiled=True)
+    on_chip = lax.psum_scatter(partial_value, "feat_core", scatter_dimension=0, tiled=True)
+    logits = sharpness * lax.psum_scatter(on_chip, "feat_chip", scatter_dimension=0, tiled=True)
 
     local_top = jnp.max(logits, axis=1)
     local_sum = jnp.sum(jnp.exp(logits - local_top[:, None]), axis=1)
@@ -43,7 +44,8 @@
     total = jnp.sum(stats[:, 1] * jnp.exp(stats[:, 0] - top_score[None, :]), axis=0)
     resp = (jnp.exp(logits - top_score[:, None]) / total[:, None]).astype(jnp.bfloat16)
 
-    group_resp = lax.all_gather(resp, "feat", axis=0, tiled=True)
+    chip_resp = lax.all_gather(resp, "feat_chip", axis=0, tiled=True)
+    group_resp = lax.all_gather(chip_resp, "feat_core", axis=0, tiled=True)
     mass_part = jnp.sum(group_resp.astype(jnp.float32), axis=0)
     sums_part = lax.dot_general(
         group_resp, group_features, (((0,), (0,)), ((), ())), preferred_element_type=jnp.float32
@@ -58,10 +60,15 @@
 
 
 def solution(mesh):
+    n_dp, n_feat, n_cent = (mesh.shape[a] for a in ("dp", "feat", "cent"))
+    split = jax.sharding.Mesh(
+        mesh.devices.reshape(n_dp, n_feat // 2, 2, n_cent), ("dp", "feat_chip", "feat_core", "cent")
+    )
+    feat = ("feat_chip", "feat_core")
     return jax.shard_map(
         shards,
-        mesh=mesh,
-        in_specs=(P(("dp", "cent"), None), P(None, "feat"), P("feat"), P("cent", "feat")),
-        out_specs=P("cent", "feat"),
+        mesh=split,
+        in_specs=(P(("dp", "cent"), None), P(None, feat), P(feat), P("cent", feat)),
+        out_specs=P("cent", feat),
         check_vma=False,
     )

time: 250 us -> 282 us (1.13)
  waiting for transfers between devices: 190 us -> 221 us
    reduce_scatter x1 -> x2, waiting for transfers between devices: 36.6 us -> 52.4 us  [the longest x1 35.4 us: shards(): lax.psum_scatter(on_chip, 'feat_chip', scatter_dimension=0, tiled=True)]
    all_gather x1 -> x2, waiting for transfers between devices: 29.7 us -> 44.8 us  [the longest x1 24.3 us: shards(): chip_resp = lax.all_gather(resp, 'feat_chip', axis=0, tiled=True)]
  transfers between devices with their start and end apart: 11 -> 13, of which waited for: 5 -> 7; matrix products, arithmetic and copies ran while one was open for 0% -> 0% of each run, Pallas kernels for 0% -> 0%
where the time goes in v3:
time: 282 us
  waiting for transfers between devices  221 us (78%)
  matrix products  17.5 us (6%)
  starting transfers between devices  15.4 us (5%)
  between operations  13.6 us (5%)
  other arithmetic  12.2 us (4%)
    psum x1, waiting for transfers between devices, shards(): both = lax.psum(jnp.concatenate([sums_part, mass_block], axis=0), 'dp')  64.9 us
    all_gather x1, waiting for transfers between devices, shards(): group_features = lax.all_gather(features, 'cent', axis=0, tiled=True)  58.2 us
    reduce_scatter x1, waiting for transfers between devices, shards(): lax.psum_scatter(on_chip, 'feat_chip', scatter_dimension=0, tiled=True)  35.4 us
    all_gather x1, waiting for transfers between devices, shards(): chip_resp = lax.all_gather(resp, 'feat_chip', axis=0, tiled=True)  24.3 us
    all_gather x1, waiting for transfers between devices, shards(): group_resp = lax.all_gather(chip_resp, 'feat_core', axis=0, tiled=True)  20.5 us
    reduce_scatter x1, waiting for transfers between devices, shards(): lax.psum_scatter(partial_value, 'feat_core', scatter_dimension=0, tiled=T...  17 us
    ppermute x7, starting transfers between devices, shards(): lax.ppermute(pair, 'cent', [(i, (i + shift) % n_cent) for i in range(n_ce...  15 us
    dot_general x1, matrix products, shards(): lax.dot_general(group_features, centroids, (((1,), (1,)), ((), ())), pref...  6.54 us
  transfers between devices with their start and end apart: 13, of which 7 were waited for; matrix products, arithmetic and copies ran while one was open for 0% of the time, Pallas kernels for 0%

profile of v3, /device:TPU:1, one launch (start us, length us, event | category | flops | bytes accessed | tf_op | source)
XLA Modules:
  0.0 281.6 jit_solution(891067852627415283)
XLA Ops:
  6.5 1.4 copy-done
  7.9 5.8 %fusion.4 = bf16[256,1024]{1,0:T(8,128)(2,1)} fusion(bf16[256,768]{1,0:T(8,128)(2,1)} %param.4, bf16[768,1024]{1,0:T(8,128)(2,1)S(1)} %copy-done, f32[1024]{0:T(1024)} %param.6), kind=kOutput, calls=%fused_computation.10 | convolution fusion | flops 403439616 | bytes 2494464 | tf_op jit(solution)/shard_map/dot_general | solution.py:17
  13.7 0.0 all-gather.4.cloned.1.call-update
  13.7 0.0 reduce-scatter.3.cloned.1.call-start
  13.8 0.3 fusion
  14.1 58.2 %all-gather.4.cloned.1.call-done = bf16[2048,1024]{1,0:T(8,128)(2,1)} async-done(((bf16[256,1024]{1,0:T(8,128)(2,1)}), bf16[2048,1024]{1,0:T(8,128)(2,1)}) %all-gather.4.cloned.1.call-update) | async-done | bytes 4194320 | tf_op jit(solution)/shard_map/all_gather | solution.py:23
  72.3 6.5 %multiply_subtract_fusion = f32[2048,512]{1,0:T(8,128)} fusion(bf16[2048,1024]{1,0:T(8,128)(2,1)} %all-gather.4.cloned.1.call-done, bf16[512,1024]{1,0:T(8,128)(2,1)S(1)} %copy-done.1, f32[512]{0:T(512)S(1)} %fusion), kind=kOutput, calls=%fused_computation.1 | convolution fusion | flops 2149580800 | bytes 9439232 | tf_op jit(solution)/shard_map/dot_general | solution.py:28
  78.8 0.0 reduce-scatter.5.cloned.1.call-start
  78.9 17.0 %reduce-scatter.3.cloned.1.call-done = f32[1024,512]{1,0:T(8,128)} async-done(((f32[2048,512]{1,0:T(8,128)}), f32[1024,512]{1,0:T(8,128)}) %reduce-scatter.3.cloned.1.call-update) | async-done | bytes 2097168 | tf_op jit(solution)/shard_map/reduce_scatter | solution.py:32
  95.9 0.0 all-gather.6.cloned.1.call-start
  95.9 35.4 %reduce-scatter.5.cloned.1.call-done = f32[256,512]{1,0:T(8,128)} async-done(((f32[1024,512]{1,0:T(8,128)}), f32[256,512]{1,0:T(8,128)}) %reduce-scatter.5.cloned.1.call-update) | async-done | bytes 524304 | tf_op jit(solution)/shard_map/reduce_scatter | solution.py:33
  131.3 1.2 multiply_reduce_fusion
  132.5 1.3 exponential_reduce_fusion
  133.7 3.9 %collective-permute-start.5 = (f32[2,256]{1,0:T(2,128)S(1)}, f32[2,256]{1,0:T(2,128)S(1)}, u32[]{:S(2)}, u32[]{:S(2)}) collective-permute-start(f32[2,256]{1,0:T(2,128)S(1)} %get-tuple-element.5), channel_id=1, source_target_pairs={{0,6},{1,7},{2,0},{3,1},{4,2},{5,3},{6,4},{7,5},{8,14},{9,15},{10,... | collective-permute-start | bytes 6152 | tf_op jit(solution)/shard_map/ppermute | solution.py:41
  137.7 1.8 collective-permute-start.4
  139.5 2.8 collective-permute-start.3
  142.2 0.4 collective-permute-start.2
  142.6 3.5 %collective-permute-start.1 = (f32[2,256]{1,0:T(2,128)S(1)}, f32[2,256]{1,0:T(2,128)S(1)}, u32[]{:S(2)}, u32[]{:S(2)}) collective-permute-start(f32[2,256]{1,0:T(2,128)S(1)} %get-tuple-element.5), channel_id=1, source_target_pairs={{0,2},{1,3},{2,4},{3,5},{4,6},{5,7},{6,0},{7,1},{8,10},{9,11},{10,... | collective-permute-start | bytes 6152 | tf_op jit(solution)/shard_map/ppermute | solution.py:41
  146.1 0.4 collective-permute-start
  146.5 2.3 collective-permute-start.6
  148.9 1.1 collective-permute-done
  150.1 1.9 divide_convert_fusion
  152.1 0.0 all-gather.8.cloned.1.call-start
  152.1 24.3 %all-gather.6.cloned.1.call-done = bf16[1024,512]{1,0:T(8,128)(2,1)} async-done(((bf16[256,512]{1,0:T(8,128)(2,1)}), bf16[1024,512]{1,0:T(8,128)(2,1)}) %all-gather.6.cloned.1.call-update) | async-done | bytes 1048592 | tf_op jit(solution)/shard_map/all_gather | solution.py:47
  176.4 0.2 all-reduce.3.cloned.1.call-start
  176.7 20.5 %all-gather.8.cloned.1.call-done = bf16[2048,512]{1,0:T(8,128)(2,1)} async-done(((bf16[1024,512]{1,0:T(8,128)(2,1)}), bf16[2048,512]{1,0:T(8,128)(2,1)}) %all-gather.8.cloned.1.call-update) | async-done | bytes 2097168 | tf_op jit(solution)/shard_map/all_gather | solution.py:48
  197.2 1.9 convert_reduce_fusion
  199.1 5.2 %fusion.9 = f32[512,1024]{1,0:T(8,128)S(1)} fusion(bf16[2048,512]{1,0:T(8,128)(2,1)} %all-gather.8.cloned.1.call-done, bf16[2048,1024]{1,0:T(8,128)(2,1)} %all-gather.4.cloned.1.call-done), kind=kOutput, calls=%fused_computation.23 | convolution fusion | flops 2147483648 | bytes 8388608 | tf_op jit(solution)/shard_map/dot_general | solution.py:50
  204.3 1.6 pad_maximum_fusion
  205.9 64.9 %all-reduce.3.cloned.1.call-done = f32[513,1024]{1,0:T(8,128)} async-done(((f32[513,1024]{1,0:T(8,128)}), f32[513,1024]{1,0:T(8,128)}) %all-reduce.3.cloned.1.call-update) | async-done | bytes 2101264 | tf_op jit(solution)/shard_map/psum | solution.py:56
  270.7 0.7 slice_add_fusion
  271.4 3.3 %fusion.1 = f32[512,1024]{1,0:T(8,128)} fusion(bf16[512,1024]{1,0:T(8,128)(2,1)S(1)} %copy-done.1, f32[513,1024]{1,0:T(8,128)} %all-reduce.3.cloned.1.call-done, f32[512]{0:T(512)S(1)} %bitcast.32), kind=kLoop, calls=%fused_computation.6 | loop fusion | flops 1572864 | bytes 5244928 | tf_op jit(solution)/shard_map/div | solution.py:59
  (28 shorter events, 0.2 us)
Async XLA Ops:
  6.5 1.4 copy-start
  6.5 7.2 %copy-start.1 = (bf16[512,1024]{1,0:T(8,128)(2,1)S(1)}, bf16[512,1024]{1,0:T(8,128)(2,1)}, u32[]{:S(2)}) copy-start(bf16[512,1024]{1,0:T(8,128)(2,1)} %param.7) | copy-start | bytes 3145732
  6.5 65.7 %all-gather.4.cloned.1.call-start = ((), (), s32[]{:S(2)}) async-start(), calls=%async_computation.2 | async-start | bytes 4718592 | tf_op jit(solution)/shard_map/all_gather | solution.py:23
  13.7 82.1 %reduce-scatter.3.cloned.1.call-start = ((), (), s32[]{:S(2)}) async-start(), calls=%async_computation.3 | async-start | bytes 6291456 | tf_op jit(solution)/shard_map/reduce_scatter | solution.py:32
  78.8 52.5 %reduce-scatter.5.cloned.1.call-start = ((), (), s32[]{:S(2)}) async-start(), calls=%async_computation.4 | async-start | bytes 2621440 | tf_op jit(solution)/shard_map/reduce_scatter | solution.py:33
  95.9 80.5 %all-gather.6.cloned.1.call-start = ((), (), s32[]{:S(2)}) async-start(), calls=%async_computation.5 | async-start | bytes 1310720 | tf_op jit(solution)/shard_map/all_gather | solution.py:47
  133.7 12.4 %collective-permute-start.5 = (f32[2,256]{1,0:T(2,128)S(1)}, f32[2,256]{1,0:T(2,128)S(1)}, u32[]{:S(2)}, u32[]{:S(2)}) collective-permute-start(f32[2,256]{1,0:T(2,128)S(1)} %get-tuple-element.5), channel_id=1, source_target_pairs={{0,6},{1,7},{2,0},{3,1},{4,2},{5,3},{6,4},{7,5},{8,14},{9,15},{10,... | collective-permute-start | bytes 6152 | tf_op jit(solution)/shard_map/ppermute | solution.py:41
  137.7 8.8 %collective-permute-start.4 = (f32[2,256]{1,0:T(2,128)S(1)}, f32[2,256]{1,0:T(2,128)S(1)}, u32[]{:S(2)}, u32[]{:S(2)}) collective-permute-start(f32[2,256]{1,0:T(2,128)S(1)} %get-tuple-element.5), channel_id=1, source_target_pairs={{0,5},{1,6},{2,7},{3,0},{4,1},{5,2},{6,3},{7,4},{8,13},{9,14},{10,... | collective-permute-start | bytes 6152 | tf_op jit(solution)/shard_map/ppermute | solution.py:41
  139.5 9.3 %collective-permute-start.3 = (f32[2,256]{1,0:T(2,128)S(1)}, f32[2,256]{1,0:T(2,128)S(1)}, u32[]{:S(2)}, u32[]{:S(2)}) collective-permute-start(f32[2,256]{1,0:T(2,128)S(1)} %get-tuple-element.5), channel_id=1, source_target_pairs={{0,4},{1,5},{2,6},{3,7},{4,0},{5,1},{6,2},{7,3},{8,12},{9,13},{10,... | collective-permute-start | bytes 6152 | tf_op jit(solution)/shard_map/ppermute | solution.py:41
  142.2 6.6 %collective-permute-start.2 = (f32[2,256]{1,0:T(2,128)S(1)}, f32[2,256]{1,0:T(2,128)S(1)}, u32[]{:S(2)}, u32[]{:S(2)}) collective-permute-start(f32[2,256]{1,0:T(2,128)S(1)} %get-tuple-element.5), channel_id=1, source_target_pairs={{0,3},{1,4},{2,5},{3,6},{4,7},{5,0},{6,1},{7,2},{8,11},{9,12},{10,... | collective-permute-start | bytes 6152 | tf_op jit(solution)/shard_map/ppermute | solution.py:41
  142.6 6.2 %collective-permute-start.1 = (f32[2,256]{1,0:T(2,128)S(1)}, f32[2,256]{1,0:T(2,128)S(1)}, u32[]{:S(2)}, u32[]{:S(2)}) collective-permute-start(f32[2,256]{1,0:T(2,128)S(1)} %get-tuple-element.5), channel_id=1, source_target_pairs={{0,2},{1,3},{2,4},{3,5},{4,6},{5,7},{6,0},{7,1},{8,10},{9,11},{10,... | collective-permute-start | bytes 6152 | tf_op jit(solution)/shard_map/ppermute | solution.py:41
  146.1 3.9 %collective-permute-start = (f32[2,256]{1,0:T(2,128)S(1)}, f32[2,256]{1,0:T(2,128)S(1)}, u32[]{:S(2)}, u32[]{:S(2)}) collective-permute-start(f32[2,256]{1,0:T(2,128)S(1)} %get-tuple-element.5), channel_id=1, source_target_pairs={{0,1},{1,2},{2,3},{3,4},{4,5},{5,6},{6,7},{7,0},{8,9},{9,10},{10,1... | collective-permute-start | bytes 6152 | tf_op jit(solution)/shard_map/ppermute | solution.py:41
  146.5 3.5 %collective-permute-start.6 = (f32[2,256]{1,0:T(2,128)S(1)}, f32[2,256]{1,0:T(2,128)S(1)}, u32[]{:S(2)}, u32[]{:S(2)}) collective-permute-start(f32[2,256]{1,0:T(2,128)S(1)} %get-tuple-element.5), channel_id=1, source_target_pairs={{0,7},{1,0},{2,1},{3,2},{4,3},{5,4},{6,5},{7,6},{8,15},{9,8},{10,9... | collective-permute-start | bytes 6152 | tf_op jit(solution)/shard_map/ppermute | solution.py:41
  152.1 45.1 %all-gather.8.cloned.1.call-start = ((), (), s32[]{:S(2)}) async-start(), calls=%async_computation.6 | async-start | bytes 3145728 | tf_op jit(solution)/shard_map/all_gather | solution.py:48
  176.4 94.3 %all-reduce.3.cloned.1.call-start = ((), (), s32[]{:S(2)}) async-start(), calls=%async_computation.7 | async-start | bytes 4259840 | tf_op jit(solution)/shard_map/psum | solution.py:56
Sparse Core Ops, SparseCore 0:
  13.8 58.3 all-gather.3
  78.9 16.8 reduce-scatter.2
  98.4 32.8 reduce-scatter.4
  152.2 24.1 all-gather.5
  178.1 19.0 all-gather.7
  206.0 64.6 all-reduce.2

commit v4 on v2

--- a/solution.py
+++ b/solution.py
@@ -48,13 +48,40 @@
     sums_part = lax.dot_general(
         group_resp, group_features, (((0,), (0,)), ((), ())), preferred_element_type=jnp.float32
     )
-    width = sums_part.shape[1]
-    mass_rows = -(-mass_part.shape[0] // width)
-    mass_block = jnp.pad(mass_part, (0, mass_rows * width - mass_part.shape[0])).reshape(mass_rows, width)
-    both = lax.psum(jnp.concatenate([sums_part, mass_block], axis=0), "dp")
-    sums = both[: sums_part.shape[0]]
-    mass = both[sums_part.shape[0] :].reshape(-1)[: mass_part.shape[0]]
-    return (sums + PRIOR_MASS * center_wide) / (mass + PRIOR_MASS)[:, None]
+    n_dp = lax.axis_size("dp")
+    me = lax.axis_index("dp")
+    n_rows, width = sums_part.shape
+    split = n_rows // 2
+    chunk = (n_rows - split) // n_dp
+
+    def as_rows(values):
+        count = -(-values.shape[-1] // width)
+        padded = jnp.pad(values, [(0, 0)] * (values.ndim - 1) + [(0, count * width - values.shape[-1])])
+        return padded.reshape(values.shape[:-1] + (count, width))
+
+    both = lax.psum(jnp.concatenate([sums_part[:split], as_rows(mass_part[:split])], axis=0), "dp")
+    mass = both[split:].reshape(-1)[:split]
+
+    pieces = jnp.concatenate(
+        [sums_part[split:].reshape(n_dp, chunk, width), as_rows(mass_part[split:].reshape(n_dp, chunk))], axis=1
+    )
+    owned = lax.dynamic_index_in_dim(pieces, me, 0, keepdims=False)
+    for shift in range(1, n_dp):
+        ring = [(i, (i + shift) % n_dp) for i in range(n_dp)]
+        outgoing = lax.dynamic_index_in_dim(pieces, (me + shift) % n_dp, 0, keepdims=False)
+        owned = owned + lax.ppermute(outgoing, "dp", ring)
+    old_owned = lax.dynamic_slice_in_dim(center_wide, split + me * chunk, chunk, 0)
+    mass_owned = owned[chunk:].reshape(-1)[:chunk]
+    fresh = (owned[:chunk] + PRIOR_MASS * old_owned) / (mass_owned + PRIOR_MASS)[:, None]
+    arrived = [fresh]
+    for shift in range(1, n_dp):
+        ring = [(i, (i + shift) % n_dp) for i in range(n_dp)]
+        arrived.append(lax.ppermute(fresh, "dp", ring))
+    order = (me - jnp.arange(n_dp)) % n_dp
+    lower = jnp.take(jnp.stack(arrived), order, axis=0).reshape(n_rows - split, width)
+
+    upper = (both[:split] + PRIOR_MASS * center_wide[:split]) / (mass + PRIOR_MASS)[:, None]
+    return jnp.concatenate([upper, lower], axis=0)
 
 
 def solution(mesh):

time: 250 us -> 252 us (level)
  waiting for transfers between devices: 190 us -> 173 us
  starting transfers between devices: 15.2 us -> 24.3 us
  other arithmetic: 12.2 us -> 17.1 us
  local copies, waits for them, and re-layouts: 1.48 us -> 5.57 us
    psum x1, waiting for transfers between devices: 64.3 us -> 20.8 us  [shards(): lax.psum(jnp.concatenate([sums_part[:split], as_rows(mass_part[:split])],...]
    ppermute x0 -> x6, waiting for transfers between devices: none -> 26.8 us  [the longest x3 18.5 us: shards(): arrived.append(lax.ppermute(fresh, 'dp', ring))]
    ppermute x0 -> x6, starting transfers between devices: none -> 9.08 us  [the longest x3 4.77 us: shards(): owned = owned + lax.ppermute(outgoing, 'dp', ring)]
  transfers between devices with their start and end apart: 11 -> 17, of which waited for: 5 -> 9; matrix products, arithmetic and copies ran while one was open for 0% -> 4% of each run, Pallas kernels for 0% -> 0%
where the time goes in v4:
time: 252 us; the launch traced here: 251 us
  waiting for transfers between devices  173 us (69%)
  starting transfers between devices  24.3 us (10%)
  matrix products  17.5 us (7%)
  other arithmetic  17.1 us (7%)
  between operations  13.3 us (5%)
  local copies, waits for them, and re-layouts  5.57 us (2%)
    all_gather x1, waiting for transfers between devices, shards(): group_features = lax.all_gather(features, 'cent', axis=0, tiled=True)  58.2 us
    reduce_scatter x1, waiting for transfers between devices, shards(): lax.psum_scatter(partial_value, 'feat', scatter_dimension=0, tiled=True)  36.6 us
    all_gather x1, waiting for transfers between devices, shards(): group_resp = lax.all_gather(resp, 'feat', axis=0, tiled=True)  30.2 us
    psum x1, waiting for transfers between devices, shards(): lax.psum(jnp.concatenate([sums_part[:split], as_rows(mass_part[:split])],...  20.8 us
    ppermute x3, waiting for transfers between devices, shards(): arrived.append(lax.ppermute(fresh, 'dp', ring))  18.5 us
    ppermute x7, starting transfers between devices, shards(): lax.ppermute(pair, 'cent', [(i, (i + shift) % n_cent) for i in range(n_ce...  14.9 us
    ppermute x3, waiting for transfers between devices, shards(): owned = owned + lax.ppermute(outgoing, 'dp', ring)  8.25 us
    dot_general x1, matrix products, shards(): lax.dot_general(group_features, centroids, (((1,), (1,)), ((), ())), pref...  6.55 us
  transfers between devices with their start and end apart: 17, of which 9 were waited for; matrix products, arithmetic and copies ran while one was open for 4% of the time, Pallas kernels for 0%

profile of v4, /device:TPU:1, one launch (start us, length us, event | category | flops | bytes accessed | tf_op | source)
XLA Modules:
  0.0 251.1 jit_solution(13001801591581583002)
XLA Ops:
  6.5 1.4 copy-done
  7.9 5.8 %fusion.2 = bf16[256,1024]{1,0:T(8,128)(2,1)} fusion(bf16[256,768]{1,0:T(8,128)(2,1)} %param.4, bf16[768,1024]{1,0:T(8,128)(2,1)S(1)} %copy-done, f32[1024]{0:T(1024)} %param.6), kind=kOutput, calls=%fused_computation.12 | convolution fusion | flops 403439616 | bytes 2494464 | tf_op jit(solution)/shard_map/dot_general | solution.py:17
  14.1 58.2 %all-gather.3.cloned.1.call-done = bf16[2048,1024]{1,0:T(8,128)(2,1)} async-done(((bf16[256,1024]{1,0:T(8,128)(2,1)}), bf16[2048,1024]{1,0:T(8,128)(2,1)}) %all-gather.3.cloned.1.call-update) | async-done | bytes 4194320 | tf_op jit(solution)/shard_map/all_gather | solution.py:23
  72.3 6.5 %multiply_subtract_fusion = f32[2048,512]{1,0:T(8,128)} fusion(bf16[2048,1024]{1,0:T(8,128)(2,1)} %all-gather.3.cloned.1.call-done, bf16[512,1024]{1,0:T(8,128)(2,1)S(1)} %copy-done.1, f32[512]{0:T(512)S(1)} %multiply_reduce_fusion), kind=kOutput, calls=%fused_computation.2 | convolution fusion | flops 2149580800 | bytes 9439232 | tf_op jit(solution)/shard_map/dot_general | solution.py:28
  78.9 36.6 %reduce-scatter.2.cloned.1.call-done = f32[256,512]{1,0:T(8,128)} async-done(((f32[2048,512]{1,0:T(8,128)}), f32[256,512]{1,0:T(8,128)}) %reduce-scatter.2.cloned.1.call-update) | async-done | bytes 524304 | tf_op jit(solution)/shard_map/reduce_scatter | solution.py:32
  115.5 1.2 multiply_reduce_fusion.1
  116.7 1.3 exponential_reduce_fusion
  118.0 5.4 %collective-permute-start.3 = (f32[2,256]{1,0:T(2,128)S(1)}, f32[2,256]{1,0:T(2,128)S(1)}, u32[]{:S(2)}, u32[]{:S(2)}) collective-permute-start(f32[2,256]{1,0:T(2,128)S(1)} %get-tuple-element.12), channel_id=1, source_target_pairs={{0,4},{1,5},{2,6},{3,7},{4,0},{5,1},{6,2},{7,3},{8,12},{9,13},{10,... | collective-permute-start | bytes 6152 | tf_op jit(solution)/shard_map/ppermute | solution.py:40
  123.4 2.9 %collective-permute-start.5 = (f32[2,256]{1,0:T(2,128)S(1)}, f32[2,256]{1,0:T(2,128)S(1)}, u32[]{:S(2)}, u32[]{:S(2)}) collective-permute-start(f32[2,256]{1,0:T(2,128)S(1)} %get-tuple-element.12), channel_id=1, source_target_pairs={{0,6},{1,7},{2,0},{3,1},{4,2},{5,3},{6,4},{7,5},{8,14},{9,15},{10,... | collective-permute-start | bytes 6152 | tf_op jit(solution)/shard_map/ppermute | solution.py:40
  127.0 3.6 %collective-permute-start.2 = (f32[2,256]{1,0:T(2,128)S(1)}, f32[2,256]{1,0:T(2,128)S(1)}, u32[]{:S(2)}, u32[]{:S(2)}) collective-permute-start(f32[2,256]{1,0:T(2,128)S(1)} %get-tuple-element.12), channel_id=1, source_target_pairs={{0,3},{1,4},{2,5},{3,6},{4,7},{5,0},{6,1},{7,2},{8,11},{9,12},{10,... | collective-permute-start | bytes 6152 | tf_op jit(solution)/shard_map/ppermute | solution.py:40
  130.6 2.3 collective-permute-start.6
  133.7 1.9 divide_convert_fusion
  135.9 30.2 %all-gather.5.cloned.1.call-done = bf16[2048,512]{1,0:T(8,128)(2,1)} async-done(((bf16[256,512]{1,0:T(8,128)(2,1)}), bf16[2048,512]{1,0:T(8,128)(2,1)}) %all-gather.5.cloned.1.call-update) | async-done | bytes 2097168 | tf_op jit(solution)/shard_map/all_gather | solution.py:46
  166.1 5.2 %fusion.26 = f32[512,1024]{1,0:T(8,128)S(1)} fusion(bf16[2048,512]{1,0:T(8,128)(2,1)} %all-gather.5.cloned.1.call-done, bf16[2048,1024]{1,0:T(8,128)(2,1)} %all-gather.3.cloned.1.call-done), kind=kOutput, calls=%fused_computation.64 | convolution fusion | flops 2147483648 | bytes 8388608 | tf_op jit(solution)/shard_map/dot_general | solution.py:48
  171.3 1.2 fusion.24
  174.7 1.2 collective-permute-start.7
  175.9 2.4 collective-permute-start.8
  178.3 1.2 collective-permute-start.9
  179.5 1.6 convert_element_type.17
  181.1 2.3 pad_maximum_fusion.1
  184.4 7.2 %collective-permute-done.8 = f32[65,1024]{1,0:T(8,128)S(1)} collective-permute-done((f32[65,1024]{1,0:T(8,128)}, f32[65,1024]{1,0:T(8,128)S(1)}, u32[]{:S(2)}, u32[]{:S(2)}) %collective-permute-start.8) | collective-permute-done | bytes 266272 | tf_op jit(solution)/shard_map/ppermute | solution.py:72
  191.8 1.1 fusion.15
  192.8 1.2 collective-permute-start.10
  194.0 2.7 %collective-permute-start.11 = (f32[64,1024]{1,0:T(8,128)S(1)}, f32[64,1024]{1,0:T(8,128)S(1)}, u32[]{:S(2)}, u32[]{:S(2)}) collective-permute-start(f32[64,1024]{1,0:T(8,128)S(1)} %fusion.15), channel_id=1, source_target_pairs={{0,128},{64,192},{128,0},{192,64},{1,129},{65,193},{129,1},{193,65... | collective-permute-start | bytes 786440 | tf_op jit(solution)/shard_map/ppermute | solution.py:79
  197.3 10.1 %collective-permute-done.10 = f32[64,1024]{1,0:T(8,128)S(1)} collective-permute-done((f32[64,1024]{1,0:T(8,128)S(1)}, f32[64,1024]{1,0:T(8,128)S(1)}, u32[]{:S(2)}, u32[]{:S(2)}) %collective-permute-start.10) | collective-permute-done | bytes 262176 | tf_op jit(solution)/shard_map/ppermute | solution.py:79
  207.4 8.4 %collective-permute-done.11 = f32[64,1024]{1,0:T(8,128)S(1)} collective-permute-done((f32[64,1024]{1,0:T(8,128)S(1)}, f32[64,1024]{1,0:T(8,128)S(1)}, u32[]{:S(2)}, u32[]{:S(2)}) %collective-permute-start.11) | collective-permute-done | bytes 262176 | tf_op jit(solution)/shard_map/ppermute | solution.py:79
  215.9 1.0 pad_maximum_fusion.2
  216.9 1.9 gather_fusion
  218.8 1.1 bitcast_select_fusion
  219.9 20.8 %all-reduce.4.cloned.1.call-done = f32[257,1024]{1,0:T(8,128)} async-done(((f32[257,1024]{1,0:T(8,128)}), f32[257,1024]{1,0:T(8,128)}) %all-reduce.4.cloned.1.call-update) | async-done | bytes 1052688 | tf_op jit(solution)/shard_map/psum | solution.py:62
  241.3 1.7 fusion.3
  243.1 1.5 pad_maximum_fusion
  (59 shorter events, 6.7 us)
Async XLA Ops:
  6.5 1.4 copy-start
  6.5 7.2 %copy-start.1 = (bf16[512,1024]{1,0:T(8,128)(2,1)S(1)}, bf16[512,1024]{1,0:T(8,128)(2,1)}, u32[]{:S(2)}) copy-start(bf16[512,1024]{1,0:T(8,128)(2,1)} %param.7) | copy-start | bytes 3145732
  6.5 65.7 %all-gather.3.cloned.1.call-start = ((), (), s32[]{:S(2)}) async-start(), calls=%async_computation.1 | async-start | bytes 4718592 | tf_op jit(solution)/shard_map/all_gather | solution.py:23
  13.7 101.8 %reduce-scatter.2.cloned.1.call-start = ((), (), s32[]{:S(2)}) async-start(), calls=%async_computation.2 | async-start | bytes 4718592 | tf_op jit(solution)/shard_map/reduce_scatter | solution.py:32
  78.8 87.3 %all-gather.5.cloned.1.call-start = ((), (), s32[]{:S(2)}) async-start(), calls=%async_computation.3 | async-start | bytes 2359296 | tf_op jit(solution)/shard_map/all_gather | solution.py:46
  118.0 9.1 %collective-permute-start.3 = (f32[2,256]{1,0:T(2,128)S(1)}, f32[2,256]{1,0:T(2,128)S(1)}, u32[]{:S(2)}, u32[]{:S(2)}) collective-permute-start(f32[2,256]{1,0:T(2,128)S(1)} %get-tuple-element.12), channel_id=1, source_target_pairs={{0,4},{1,5},{2,6},{3,7},{4,0},{5,1},{6,2},{7,3},{8,12},{9,13},{10,... | collective-permute-start | bytes 6152 | tf_op jit(solution)/shard_map/ppermute | solution.py:40
  123.4 7.2 %collective-permute-start.4 = (f32[2,256]{1,0:T(2,128)S(1)}, f32[2,256]{1,0:T(2,128)S(1)}, u32[]{:S(2)}, u32[]{:S(2)}) collective-permute-start(f32[2,256]{1,0:T(2,128)S(1)} %get-tuple-element.12), channel_id=1, source_target_pairs={{0,5},{1,6},{2,7},{3,0},{4,1},{5,2},{6,3},{7,4},{8,13},{9,14},{10,... | collective-permute-start | bytes 6152 | tf_op jit(solution)/shard_map/ppermute | solution.py:40
  123.4 9.5 %collective-permute-start.5 = (f32[2,256]{1,0:T(2,128)S(1)}, f32[2,256]{1,0:T(2,128)S(1)}, u32[]{:S(2)}, u32[]{:S(2)}) collective-permute-start(f32[2,256]{1,0:T(2,128)S(1)} %get-tuple-element.12), channel_id=1, source_target_pairs={{0,6},{1,7},{2,0},{3,1},{4,2},{5,3},{6,4},{7,5},{8,14},{9,15},{10,... | collective-permute-start | bytes 6152 | tf_op jit(solution)/shard_map/ppermute | solution.py:40
  126.3 6.6 %collective-permute-start = (f32[2,256]{1,0:T(2,128)S(1)}, f32[2,256]{1,0:T(2,128)S(1)}, u32[]{:S(2)}, u32[]{:S(2)}) collective-permute-start(f32[2,256]{1,0:T(2,128)S(1)} %get-tuple-element.12), channel_id=1, source_target_pairs={{0,1},{1,2},{2,3},{3,4},{4,5},{5,6},{6,7},{7,0},{8,9},{9,10},{10,1... | collective-permute-start | bytes 6152 | tf_op jit(solution)/shard_map/ppermute | solution.py:40
  126.3 6.6 %collective-permute-start.1 = (f32[2,256]{1,0:T(2,128)S(1)}, f32[2,256]{1,0:T(2,128)S(1)}, u32[]{:S(2)}, u32[]{:S(2)}) collective-permute-start(f32[2,256]{1,0:T(2,128)S(1)} %get-tuple-element.12), channel_id=1, source_target_pairs={{0,2},{1,3},{2,4},{3,5},{4,6},{5,7},{6,0},{7,1},{8,10},{9,11},{10,... | collective-permute-start | bytes 6152 | tf_op jit(solution)/shard_map/ppermute | solution.py:40
  127.0 6.0 %collective-permute-start.2 = (f32[2,256]{1,0:T(2,128)S(1)}, f32[2,256]{1,0:T(2,128)S(1)}, u32[]{:S(2)}, u32[]{:S(2)}) collective-permute-start(f32[2,256]{1,0:T(2,128)S(1)} %get-tuple-element.12), channel_id=1, source_target_pairs={{0,3},{1,4},{2,5},{3,6},{4,7},{5,0},{6,1},{7,2},{8,11},{9,12},{10,... | collective-permute-start | bytes 6152 | tf_op jit(solution)/shard_map/ppermute | solution.py:40
  130.6 3.0 %collective-permute-start.6 = (f32[2,256]{1,0:T(2,128)S(1)}, f32[2,256]{1,0:T(2,128)S(1)}, u32[]{:S(2)}, u32[]{:S(2)}) collective-permute-start(f32[2,256]{1,0:T(2,128)S(1)} %get-tuple-element.12), channel_id=1, source_target_pairs={{0,7},{1,0},{2,1},{3,2},{4,3},{5,4},{6,5},{7,6},{8,15},{9,8},{10,9... | collective-permute-start | bytes 6152 | tf_op jit(solution)/shard_map/ppermute | solution.py:40
  135.7 105.0 %all-reduce.4.cloned.1.call-start = ((), (), s32[]{:S(2)}) async-start(), calls=%async_computation.4 | async-start | bytes 2162688 | tf_op jit(solution)/shard_map/psum | solution.py:62
  171.3 2.0 copy-start.4
  173.7 5.8 %copy-start.2 = (bf16[512,1024]{1,0:T(8,128)(2,1)S(1)}, bf16[512,1024]{1,0:T(8,128)(2,1)}, u32[]{:S(2)}) copy-start(bf16[512,1024]{1,0:T(8,128)(2,1)} %param.7) | copy-start | bytes 3145732
  174.7 9.7 %collective-permute-start.7 = (f32[65,1024]{1,0:T(8,128)}, f32[65,1024]{1,0:T(8,128)S(1)}, u32[]{:S(2)}, u32[]{:S(2)}) collective-permute-start(f32[65,1024]{1,0:T(8,128)} %get-tuple-element.7), channel_id=1, source_target_pairs={{0,64},{64,128},{128,192},{192,0},{1,65},{65,129},{129,193},{193,1... | collective-permute-start | bytes 798728 | tf_op jit(solution)/shard_map/ppermute | solution.py:72
  175.9 15.8 %collective-permute-start.8 = (f32[65,1024]{1,0:T(8,128)}, f32[65,1024]{1,0:T(8,128)S(1)}, u32[]{:S(2)}, u32[]{:S(2)}) collective-permute-start(f32[65,1024]{1,0:T(8,128)} %get-tuple-element.8), channel_id=1, source_target_pairs={{0,128},{64,192},{128,0},{192,64},{1,129},{65,193},{129,1},{193,65... | collective-permute-start | bytes 798728 | tf_op jit(solution)/shard_map/ppermute | solution.py:72
  178.3 13.4 %collective-permute-start.9 = (f32[65,1024]{1,0:T(8,128)}, f32[65,1024]{1,0:T(8,128)S(1)}, u32[]{:S(2)}, u32[]{:S(2)}) collective-permute-start(f32[65,1024]{1,0:T(8,128)} %get-tuple-element.9), channel_id=1, source_target_pairs={{0,192},{64,0},{128,64},{192,128},{1,193},{65,1},{129,65},{193,129... | collective-permute-start | bytes 798728 | tf_op jit(solution)/shard_map/ppermute | solution.py:72
  192.8 14.6 %collective-permute-start.10 = (f32[64,1024]{1,0:T(8,128)S(1)}, f32[64,1024]{1,0:T(8,128)S(1)}, u32[]{:S(2)}, u32[]{:S(2)}) collective-permute-start(f32[64,1024]{1,0:T(8,128)S(1)} %fusion.15), channel_id=1, source_target_pairs={{0,64},{64,128},{128,192},{192,0},{1,65},{65,129},{129,193},{193,1... | collective-permute-start | bytes 786440 | tf_op jit(solution)/shard_map/ppermute | solution.py:79
  194.0 21.8 %collective-permute-start.11 = (f32[64,1024]{1,0:T(8,128)S(1)}, f32[64,1024]{1,0:T(8,128)S(1)}, u32[]{:S(2)}, u32[]{:S(2)}) collective-permute-start(f32[64,1024]{1,0:T(8,128)S(1)} %fusion.15), channel_id=1, source_target_pairs={{0,128},{64,192},{128,0},{192,64},{1,129},{65,193},{129,1},{193,65... | collective-permute-start | bytes 786440 | tf_op jit(solution)/shard_map/ppermute | solution.py:79
  196.8 19.1 %collective-permute-start.12 = (f32[64,1024]{1,0:T(8,128)S(1)}, f32[64,1024]{1,0:T(8,128)S(1)}, u32[]{:S(2)}, u32[]{:S(2)}) collective-permute-start(f32[64,1024]{1,0:T(8,128)S(1)} %fusion.15), channel_id=1, source_target_pairs={{0,192},{64,0},{128,64},{192,128},{1,193},{65,1},{129,65},{193,129... | collective-permute-start | bytes 786440 | tf_op jit(solution)/shard_map/ppermute | solution.py:79
  219.9 23.2 %copy-start.3 = (f32[256,1024]{1,0:T(8,128)S(1)}, f32[256,1024]{1,0:T(8,128)}, u32[]{:S(2)}) copy-start(f32[256,1024]{1,0:T(8,128)} %bitcast_select_fusion) | copy-start | bytes 3145732
Sparse Core Ops, SparseCore 0:
  13.8 58.3 all-gather.2
  79.0 36.5 reduce-scatter.1
  135.8 30.2 all-gather.4
  183.5 57.0 all-reduce.3

commit v5 on v4

--- a/solution.py
+++ b/solution.py
@@ -45,13 +45,16 @@
 
     group_resp = lax.all_gather(resp, "feat", axis=0, tiled=True)
     mass_part = jnp.sum(group_resp.astype(jnp.float32), axis=0)
-    sums_part = lax.dot_general(
-        group_resp, group_features, (((0,), (0,)), ((), ())), preferred_element_type=jnp.float32
-    )
+    n_rows = group_resp.shape[1]
+    split = n_rows // 4
+    width = group_features.shape[1]
+
+    def row_contract(weights):
+        return lax.dot_general(
+            weights, group_features, (((0,), (0,)), ((), ())), preferred_element_type=jnp.float32
+        )
     n_dp = lax.axis_size("dp")
     me = lax.axis_index("dp")
-    n_rows, width = sums_part.shape
-    split = n_rows // 2
     chunk = (n_rows - split) // n_dp
 
     def as_rows(values):
@@ -59,11 +62,11 @@
         padded = jnp.pad(values, [(0, 0)] * (values.ndim - 1) + [(0, count * width - values.shape[-1])])
         return padded.reshape(values.shape[:-1] + (count, width))
 
-    both = lax.psum(jnp.concatenate([sums_part[:split], as_rows(mass_part[:split])], axis=0), "dp")
+    both = lax.psum(jnp.concatenate([row_contract(group_resp[:, :split]), as_rows(mass_part[:split])], axis=0), "dp")
     mass = both[split:].reshape(-1)[:split]
 
     pieces = jnp.concatenate(
-        [sums_part[split:].reshape(n_dp, chunk, width), as_rows(mass_part[split:].reshape(n_dp, chunk))], axis=1
+        [row_contract(group_resp[:, split:]).reshape(n_dp, chunk, width), as_rows(mass_part[split:].reshape(n_dp, chunk))], axis=1
     )
     owned = lax.dynamic_index_in_dim(pieces, me, 0, keepdims=False)
     for shift in range(1, n_dp):

time: 252 us -> 247 us (0.980)
  waiting for transfers between devices: 173 us -> 164 us
  other arithmetic: 17.1 us -> 19.9 us
    ppermute x3, waiting for transfers between devices: 18.5 us -> 0.01 us  [shards(): arrived.append(lax.ppermute(fresh, 'dp', ring))]
    ppermute x3, waiting for transfers between devices: 8.25 us -> 17.2 us  [shards(): owned = owned + lax.ppermute(outgoing, 'dp', ring)]
    dot_general x1 -> x2, matrix products: 5.16 us -> 6.42 us  [row_contract(): lax.dot_general(weights, group_features, (((0,), (0,)), ((), ())), prefer...]
  transfers between devices with their start and end apart: 17 -> 17, of which waited for: 9 -> 8; matrix products, arithmetic and copies ran while one was open for 4% -> 4% of each run, Pallas kernels for 0% -> 0%
where the time goes in v5:
time: 247 us; the launch traced here: 246 us
  waiting for transfers between devices  164 us (66%)
  starting transfers between devices  25.2 us (10%)
  other arithmetic  19.9 us (8%)
  matrix products  18.7 us (8%)
  between operations  13.3 us (5%)
  local copies, waits for them, and re-layouts  4.52 us (2%)
    all_gather x1, waiting for transfers between devices, shards(): group_features = lax.all_gather(features, 'cent', axis=0, tiled=True)  58.2 us
    reduce_scatter x1, waiting for transfers between devices, shards(): lax.psum_scatter(partial_value, 'feat', scatter_dimension=0, tiled=True)  36.6 us
    all_gather x1, waiting for transfers between devices, shards(): group_resp = lax.all_gather(resp, 'feat', axis=0, tiled=True)  28.5 us
    psum x1, waiting for transfers between devices, shards(): lax.psum(jnp.concatenate([row_contract(group_resp[:, :split]), as_rows(ma...  23.1 us
    ppermute x3, waiting for transfers between devices, shards(): owned = owned + lax.ppermute(outgoing, 'dp', ring)  17.2 us
    ppermute x7, starting transfers between devices, shards(): lax.ppermute(pair, 'cent', [(i, (i + shift) % n_cent) for i in range(n_ce...  14.9 us
    dot_general x1, matrix products, shards(): lax.dot_general(group_features, centroids, (((1,), (1,)), ((), ())), pref...  6.55 us
    dot_general x2, matrix products, row_contract(): lax.dot_general(weights, group_features, (((0,), (0,)), ((), ())), prefer...  6.42 us
  transfers between devices with their start and end apart: 17, of which 8 were waited for; matrix products, arithmetic and copies ran while one was open for 4% of the time, Pallas kernels for 0%

profile of v5, /device:TPU:1, one launch (start us, length us, event | category | flops | bytes accessed | tf_op | source)
XLA Modules:
  0.0 246.1 jit_solution(4010304777453575741)
XLA Ops:
  6.5 1.4 copy-done
  7.9 5.8 %fusion.4 = bf16[256,1024]{1,0:T(8,128)(2,1)} fusion(bf16[256,768]{1,0:T(8,128)(2,1)} %param.4, bf16[768,1024]{1,0:T(8,128)(2,1)S(1)} %copy-done, f32[1024]{0:T(1024)} %param.6), kind=kOutput, calls=%fused_computation.20 | convolution fusion | flops 403439616 | bytes 2494464 | tf_op jit(solution)/shard_map/dot_general | solution.py:17
  14.1 58.2 %all-gather.3.cloned.1.call-done = bf16[2048,1024]{1,0:T(8,128)(2,1)} async-done(((bf16[256,1024]{1,0:T(8,128)(2,1)}), bf16[2048,1024]{1,0:T(8,128)(2,1)}) %all-gather.3.cloned.1.call-update) | async-done | bytes 4194320 | tf_op jit(solution)/shard_map/all_gather | solution.py:23
  72.3 6.5 %multiply_subtract_fusion = f32[2048,512]{1,0:T(8,128)} fusion(bf16[2048,1024]{1,0:T(8,128)(2,1)} %all-gather.3.cloned.1.call-done, bf16[512,1024]{1,0:T(8,128)(2,1)S(1)} %copy-done.2, f32[512]{0:T(512)S(1)} %multiply_reduce_fusion), kind=kOutput, calls=%fused_computation.2 | convolution fusion | flops 2149580800 | bytes 9439232 | tf_op jit(solution)/shard_map/dot_general | solution.py:28
  78.9 36.6 %reduce-scatter.2.cloned.1.call-done = f32[256,512]{1,0:T(8,128)} async-done(((f32[2048,512]{1,0:T(8,128)}), f32[256,512]{1,0:T(8,128)}) %reduce-scatter.2.cloned.1.call-update) | async-done | bytes 524304 | tf_op jit(solution)/shard_map/reduce_scatter | solution.py:32
  115.5 1.2 multiply_reduce_fusion.1
  116.7 1.3 exponential_reduce_fusion
  118.0 5.4 %collective-permute-start.3 = (f32[2,256]{1,0:T(2,128)S(1)}, f32[2,256]{1,0:T(2,128)S(1)}, u32[]{:S(2)}, u32[]{:S(2)}) collective-permute-start(f32[2,256]{1,0:T(2,128)S(1)} %get-tuple-element.8), channel_id=1, source_target_pairs={{0,4},{1,5},{2,6},{3,7},{4,0},{5,1},{6,2},{7,3},{8,12},{9,13},{10,... | collective-permute-start | bytes 6152 | tf_op jit(solution)/shard_map/ppermute | solution.py:40
  123.4 2.9 %collective-permute-start.5 = (f32[2,256]{1,0:T(2,128)S(1)}, f32[2,256]{1,0:T(2,128)S(1)}, u32[]{:S(2)}, u32[]{:S(2)}) collective-permute-start(f32[2,256]{1,0:T(2,128)S(1)} %get-tuple-element.8), channel_id=1, source_target_pairs={{0,6},{1,7},{2,0},{3,1},{4,2},{5,3},{6,4},{7,5},{8,14},{9,15},{10,... | collective-permute-start | bytes 6152 | tf_op jit(solution)/shard_map/ppermute | solution.py:40
  127.0 3.6 %collective-permute-start.2 = (f32[2,256]{1,0:T(2,128)S(1)}, f32[2,256]{1,0:T(2,128)S(1)}, u32[]{:S(2)}, u32[]{:S(2)}) collective-permute-start(f32[2,256]{1,0:T(2,128)S(1)} %get-tuple-element.8), channel_id=1, source_target_pairs={{0,3},{1,4},{2,5},{3,6},{4,7},{5,0},{6,1},{7,2},{8,11},{9,12},{10,... | collective-permute-start | bytes 6152 | tf_op jit(solution)/shard_map/ppermute | solution.py:40
  130.6 2.3 collective-permute-start.6
  133.7 1.9 divide_convert_fusion
  135.9 1.6 convert_element_type.17
  137.7 28.5 %all-gather.5.cloned.1.call-done = bf16[2048,512]{1,0:T(8,128)(2,1)} async-done(((bf16[256,512]{1,0:T(8,128)(2,1)}), bf16[2048,512]{1,0:T(8,128)(2,1)}) %all-gather.5.cloned.1.call-update) | async-done | bytes 2097168 | tf_op jit(solution)/shard_map/all_gather | solution.py:46
  166.1 1.9 convert_reduce_fusion
  168.2 4.6 %fusion = f32[384,1024]{1,0:T(8,128)S(1)} fusion(bf16[2048,1024]{1,0:T(8,128)(2,1)} %all-gather.3.cloned.1.call-done, bf16[2048,512]{1,0:T(8,128)(2,1)} %all-gather.5.cloned.1.call-done), kind=kOutput, calls=%fused_computation.13 | convolution fusion | flops 1610612736 | bytes 7340032 | tf_op jit(solution)/shard_map/dot_general | solution.py:53
  172.8 1.1 fusion.16
  174.0 1.2 collective-permute-start.7
  175.1 2.4 collective-permute-start.8
  177.5 1.2 collective-permute-start.9
  178.7 1.8 fusion.6
  181.4 5.1 %collective-permute-done.7 = f32[97,1024]{1,0:T(8,128)} collective-permute-done((f32[97,1024]{1,0:T(8,128)}, f32[97,1024]{1,0:T(8,128)}, u32[]{:S(2)}, u32[]{:S(2)}) %collective-permute-start.7) | collective-permute-done | bytes 397344 | tf_op jit(solution)/shard_map/ppermute | solution.py:75
  186.6 11.9 %collective-permute-done.8 = f32[97,1024]{1,0:T(8,128)} collective-permute-done((f32[97,1024]{1,0:T(8,128)}, f32[97,1024]{1,0:T(8,128)}, u32[]{:S(2)}, u32[]{:S(2)}) %collective-permute-start.8) | collective-permute-done | bytes 397344 | tf_op jit(solution)/shard_map/ppermute | solution.py:75
  198.7 1.4 fusion.14
  201.2 1.8 collective-permute-start.10
  203.0 3.0 %collective-permute-start.11 = (f32[96,1024]{1,0:T(8,128)S(1)}, f32[96,1024]{1,0:T(8,128)S(1)}, u32[]{:S(2)}, u32[]{:S(2)}) collective-permute-start(f32[96,1024]{1,0:T(8,128)S(1)} %fusion.19), channel_id=1, source_target_pairs={{0,128},{64,192},{128,0},{192,64},{1,129},{65,193},{129,1},{193,65... | collective-permute-start | bytes 1179656 | tf_op jit(solution)/shard_map/ppermute | solution.py:82
  206.4 23.1 %all-reduce.4.cloned.1.call-done = f32[129,1024]{1,0:T(8,128)} async-done(((f32[129,1024]{1,0:T(8,128)}), f32[129,1024]{1,0:T(8,128)}) %all-reduce.4.cloned.1.call-update) | async-done | bytes 528400 | tf_op jit(solution)/shard_map/psum | solution.py:65
  230.2 2.1 fusion.5
  233.3 1.3 pad_maximum_fusion.1
  234.7 1.8 gather_fusion
  236.5 1.6 bitcast_select_fusion
  238.1 1.5 pad_maximum_fusion
  (64 shorter events, 6.8 us)
Async XLA Ops:
  6.5 1.4 copy-start
  6.5 7.2 %copy-start.2 = (bf16[512,1024]{1,0:T(8,128)(2,1)S(1)}, bf16[512,1024]{1,0:T(8,128)(2,1)}, u32[]{:S(2)}) copy-start(bf16[512,1024]{1,0:T(8,128)(2,1)} %param.7) | copy-start | bytes 3145732
  6.5 65.7 %all-gather.3.cloned.1.call-start = ((), (), s32[]{:S(2)}) async-start(), calls=%async_computation.1 | async-start | bytes 4718592 | tf_op jit(solution)/shard_map/all_gather | solution.py:23
  13.7 101.8 %reduce-scatter.2.cloned.1.call-start = ((), (), s32[]{:S(2)}) async-start(), calls=%async_computation.2 | async-start | bytes 4718592 | tf_op jit(solution)/shard_map/reduce_scatter | solution.py:32
  78.8 87.3 %all-gather.5.cloned.1.call-start = ((), (), s32[]{:S(2)}) async-start(), calls=%async_computation.3 | async-start | bytes 2359296 | tf_op jit(solution)/shard_map/all_gather | solution.py:46
  118.0 9.1 %collective-permute-start.3 = (f32[2,256]{1,0:T(2,128)S(1)}, f32[2,256]{1,0:T(2,128)S(1)}, u32[]{:S(2)}, u32[]{:S(2)}) collective-permute-start(f32[2,256]{1,0:T(2,128)S(1)} %get-tuple-element.8), channel_id=1, source_target_pairs={{0,4},{1,5},{2,6},{3,7},{4,0},{5,1},{6,2},{7,3},{8,12},{9,13},{10,... | collective-permute-start | bytes 6152 | tf_op jit(solution)/shard_map/ppermute | solution.py:40
  123.4 7.2 %collective-permute-start.4 = (f32[2,256]{1,0:T(2,128)S(1)}, f32[2,256]{1,0:T(2,128)S(1)}, u32[]{:S(2)}, u32[]{:S(2)}) collective-permute-start(f32[2,256]{1,0:T(2,128)S(1)} %get-tuple-element.8), channel_id=1, source_target_pairs={{0,5},{1,6},{2,7},{3,0},{4,1},{5,2},{6,3},{7,4},{8,13},{9,14},{10,... | collective-permute-start | bytes 6152 | tf_op jit(solution)/shard_map/ppermute | solution.py:40
  123.4 9.5 %collective-permute-start.5 = (f32[2,256]{1,0:T(2,128)S(1)}, f32[2,256]{1,0:T(2,128)S(1)}, u32[]{:S(2)}, u32[]{:S(2)}) collective-permute-start(f32[2,256]{1,0:T(2,128)S(1)} %get-tuple-element.8), channel_id=1, source_target_pairs={{0,6},{1,7},{2,0},{3,1},{4,2},{5,3},{6,4},{7,5},{8,14},{9,15},{10,... | collective-permute-start | bytes 6152 | tf_op jit(solution)/shard_map/ppermute | solution.py:40
  126.3 6.6 %collective-permute-start = (f32[2,256]{1,0:T(2,128)S(1)}, f32[2,256]{1,0:T(2,128)S(1)}, u32[]{:S(2)}, u32[]{:S(2)}) collective-permute-start(f32[2,256]{1,0:T(2,128)S(1)} %get-tuple-element.8), channel_id=1, source_target_pairs={{0,1},{1,2},{2,3},{3,4},{4,5},{5,6},{6,7},{7,0},{8,9},{9,10},{10,1... | collective-permute-start | bytes 6152 | tf_op jit(solution)/shard_map/ppermute | solution.py:40
  126.3 6.6 %collective-permute-start.1 = (f32[2,256]{1,0:T(2,128)S(1)}, f32[2,256]{1,0:T(2,128)S(1)}, u32[]{:S(2)}, u32[]{:S(2)}) collective-permute-start(f32[2,256]{1,0:T(2,128)S(1)} %get-tuple-element.8), channel_id=1, source_target_pairs={{0,2},{1,3},{2,4},{3,5},{4,6},{5,7},{6,0},{7,1},{8,10},{9,11},{10,... | collective-permute-start | bytes 6152 | tf_op jit(solution)/shard_map/ppermute | solution.py:40
  127.0 6.0 %collective-permute-start.2 = (f32[2,256]{1,0:T(2,128)S(1)}, f32[2,256]{1,0:T(2,128)S(1)}, u32[]{:S(2)}, u32[]{:S(2)}) collective-permute-start(f32[2,256]{1,0:T(2,128)S(1)} %get-tuple-element.8), channel_id=1, source_target_pairs={{0,3},{1,4},{2,5},{3,6},{4,7},{5,0},{6,1},{7,2},{8,11},{9,12},{10,... | collective-permute-start | bytes 6152 | tf_op jit(solution)/shard_map/ppermute | solution.py:40
  130.6 3.0 %collective-permute-start.6 = (f32[2,256]{1,0:T(2,128)S(1)}, f32[2,256]{1,0:T(2,128)S(1)}, u32[]{:S(2)}, u32[]{:S(2)}) collective-permute-start(f32[2,256]{1,0:T(2,128)S(1)} %get-tuple-element.8), channel_id=1, source_target_pairs={{0,7},{1,0},{2,1},{3,2},{4,3},{5,4},{6,5},{7,6},{8,15},{9,8},{10,9... | collective-permute-start | bytes 6152 | tf_op jit(solution)/shard_map/ppermute | solution.py:40
  135.7 93.8 %all-reduce.4.cloned.1.call-start = ((), (), s32[]{:S(2)}) async-start(), calls=%async_computation.4 | async-start | bytes 1114112 | tf_op jit(solution)/shard_map/psum | solution.py:65
  168.2 10.5 %copy-start.1 = (bf16[2048,1024]{1,0:T(8,128)(2,1)S(1)}, bf16[2048,1024]{1,0:T(8,128)(2,1)}, u32[]{:S(2)}) copy-start(bf16[2048,1024]{1,0:T(8,128)(2,1)} %all-gather.3.cloned.1.call-done) | copy-start | bytes 12582916
  174.0 12.6 %collective-permute-start.7 = (f32[97,1024]{1,0:T(8,128)}, f32[97,1024]{1,0:T(8,128)}, u32[]{:S(2)}, u32[]{:S(2)}) collective-permute-start(f32[97,1024]{1,0:T(8,128)} %get-tuple-element.5), channel_id=1, source_target_pairs={{0,64},{64,128},{128,192},{192,0},{1,65},{65,129},{129,193},{193,1... | collective-permute-start | bytes 1191944 | tf_op jit(solution)/shard_map/ppermute | solution.py:75
  175.1 23.4 %collective-permute-start.8 = (f32[97,1024]{1,0:T(8,128)}, f32[97,1024]{1,0:T(8,128)}, u32[]{:S(2)}, u32[]{:S(2)}) collective-permute-start(f32[97,1024]{1,0:T(8,128)} %get-tuple-element.6), channel_id=1, source_target_pairs={{0,128},{64,192},{128,0},{192,64},{1,129},{65,193},{129,1},{193,65... | collective-permute-start | bytes 1191944 | tf_op jit(solution)/shard_map/ppermute | solution.py:75
  177.5 21.1 %collective-permute-start.9 = (f32[97,1024]{1,0:T(8,128)}, f32[97,1024]{1,0:T(8,128)}, u32[]{:S(2)}, u32[]{:S(2)}) collective-permute-start(f32[97,1024]{1,0:T(8,128)} %get-tuple-element.7), channel_id=1, source_target_pairs={{0,192},{64,0},{128,64},{192,128},{1,193},{65,1},{129,65},{193,129... | collective-permute-start | bytes 1191944 | tf_op jit(solution)/shard_map/ppermute | solution.py:75
  201.2 31.1 %collective-permute-start.10 = (f32[96,1024]{1,0:T(8,128)S(1)}, f32[96,1024]{1,0:T(8,128)S(1)}, u32[]{:S(2)}, u32[]{:S(2)}) collective-permute-start(f32[96,1024]{1,0:T(8,128)S(1)} %fusion.19), channel_id=1, source_target_pairs={{0,64},{64,128},{128,192},{192,0},{1,65},{65,129},{129,193},{193,1... | collective-permute-start | bytes 1179656 | tf_op jit(solution)/shard_map/ppermute | solution.py:82
  203.0 29.4 %collective-permute-start.11 = (f32[96,1024]{1,0:T(8,128)S(1)}, f32[96,1024]{1,0:T(8,128)S(1)}, u32[]{:S(2)}, u32[]{:S(2)}) collective-permute-start(f32[96,1024]{1,0:T(8,128)S(1)} %fusion.19), channel_id=1, source_target_pairs={{0,128},{64,192},{128,0},{192,64},{1,129},{65,193},{129,1},{193,65... | collective-permute-start | bytes 1179656 | tf_op jit(solution)/shard_map/ppermute | solution.py:82
  205.9 26.4 %collective-permute-start.12 = (f32[96,1024]{1,0:T(8,128)S(1)}, f32[96,1024]{1,0:T(8,128)S(1)}, u32[]{:S(2)}, u32[]{:S(2)}) collective-permute-start(f32[96,1024]{1,0:T(8,128)S(1)} %fusion.19), channel_id=1, source_target_pairs={{0,192},{64,0},{128,64},{192,128},{1,193},{65,1},{129,65},{193,129... | collective-permute-start | bytes 1179656 | tf_op jit(solution)/shard_map/ppermute | solution.py:82
  232.3 0.8 copy-start.4
  232.3 0.9 copy-start.5
  232.3 1.0 copy-start.6
  236.4 1.6 copy-start.3
Sparse Core Ops, SparseCore 0:
  13.8 58.3 all-gather.2
  79.0 36.5 reduce-scatter.1
  135.8 30.2 all-gather.4
  181.6 47.9 all-reduce.3

commit v6 on v5

--- a/solution.py
+++ b/solution.py
@@ -20,7 +20,25 @@
 
 def shards(embeddings, projection, phases, centroids):
     features = featurize(embeddings, projection, phases)
-    group_features = lax.all_gather(features, "cent", axis=0, tiled=True)
+    n_cent = lax.axis_size("cent")
+    me_cent = lax.axis_index("cent")
+    half = features.shape[1] // 2
+    by_sc = lax.all_gather(features[:, :half], "cent", axis=0, tiled=True)
+    own = features[:, half:]
+    to_right = [(i, (i + 1) % n_cent) for i in range(n_cent)]
+    to_left = [(i, (i - 1) % n_cent) for i in range(n_cent)]
+    from_left, from_right = [own], []
+    moving_right, moving_left = own, own
+    for step in range(1, n_cent // 2 + 1):
+        moving_right = lax.ppermute(moving_right, "cent", to_right)
+        from_left.append(moving_right)
+        if step < n_cent - step:
+            moving_left = lax.ppermute(moving_left, "cent", to_left)
+            from_right.append(moving_left)
+    arrived = jnp.stack(from_left + from_right[::-1])
+    order = (me_cent - jnp.arange(n_cent)) % n_cent
+    by_ring = jnp.take(arrived, order, axis=0).reshape(-1, own.shape[1])
+    group_features = jnp.concatenate([by_sc, by_ring], axis=1)
     sharpness = SHARP_FACTOR / math.sqrt(F)
 
     center_wide = centroids.astype(jnp.float32)
@@ -34,7 +52,6 @@
     local_top = jnp.max(logits, axis=1)
     local_sum = jnp.sum(jnp.exp(logits - local_top[:, None]), axis=1)
     pair = jnp.stack([local_top, local_sum])
-    n_cent = lax.axis_size("cent")
     received = [pair]
     for shift in range(1, n_cent):
         received.append(lax.ppermute(pair, "cent", [(i, (i + shift) % n_cent) for i in range(n_cent)]))

time: 247 us -> 253 us (1.024)
  waiting for transfers between devices: 164 us -> 143 us
  local copies, waits for them, and re-layouts: 4.52 us -> 16.7 us
  starting transfers between devices: 25.2 us -> 37.1 us
  other arithmetic: 19.9 us -> 22.7 us
    all_gather x1, waiting for transfers between devices: 58.2 us -> 0.01 us  [shards(): by_sc = lax.all_gather(features[:, :half], 'cent', axis=0, tiled=True)]
    ppermute x0 -> x7, waiting for transfers between devices: none -> 32.9 us  [the longest x4 32.9 us: shards(): moving_right = lax.ppermute(moving_right, 'cent', to_right)]
    ppermute x0 -> x7, starting transfers between devices: none -> 12 us  [the longest x3 9.46 us: shards(): moving_left = lax.ppermute(moving_left, 'cent', to_left)]
    unnamed x14 -> x23, local copies, waits for them, and re-layouts: 2.39 us -> 9.33 us
    reduce_scatter x1, waiting for transfers between devices: 36.6 us -> 40.6 us  [shards(): lax.psum_scatter(partial_value, 'feat', scatter_dimension=0, tiled=True)]
    gather x0 -> x1, local copies, waits for them, and re-layouts: none -> 3.61 us  [shards(): by_ring = jnp.take(arrived, order, axis=0).reshape(-1, own.shape[1])]
    select_n x0 -> x2, other arithmetic: none -> 2.76 us  [shards(): by_ring = jnp.take(arrived, order, axis=0).reshape(-1, own.shape[1])]
  transfers between devices with their start and end apart: 17 -> 24, of which waited for: 8 -> 11; matrix products, arithmetic and copies ran while one was open for 4% -> 10% of each run, Pallas kernels for 0% -> 0%
where the time goes in v6:
time: 253 us; the launch traced here: 252 us
  waiting for transfers between devices  143 us (57%)
  starting transfers between devices  37.1 us (15%)
  other arithmetic  22.7 us (9%)
  matrix products  18.4 us (7%)
  local copies, waits for them, and re-layouts  16.7 us (7%)
  between operations  13.4 us (5%)
    reduce_scatter x1, waiting for transfers between devices, shards(): lax.psum_scatter(partial_value, 'feat', scatter_dimension=0, tiled=True)  40.6 us
    ppermute x4, waiting for transfers between devices, shards(): moving_right = lax.ppermute(moving_right, 'cent', to_right)  32.9 us
    all_gather x1, waiting for transfers between devices, shards(): group_resp = lax.all_gather(resp, 'feat', axis=0, tiled=True)  28.7 us
    psum x1, waiting for transfers between devices, shards(): lax.psum(jnp.concatenate([row_contract(group_resp[:, :split]), as_rows(ma...  23.1 us
    ppermute x3, waiting for transfers between devices, shards(): owned = owned + lax.ppermute(outgoing, 'dp', ring)  17.3 us
    ppermute x7, starting transfers between devices, shards(): lax.ppermute(pair, 'cent', [(i, (i + shift) % n_cent) for i in range(n_ce...  14.9 us
    ppermute x3, starting transfers between devices, shards(): moving_left = lax.ppermute(moving_left, 'cent', to_left)  9.46 us
    unnamed x23, local copies, waits for them, and re-layouts  9.33 us
  transfers between devices with their start and end apart: 24, of which 11 were waited for; matrix products, arithmetic and copies ran while one was open for 10% of the time, Pallas kernels for 0%

profile of v6, /device:TPU:1, one launch (start us, length us, event | category | flops | bytes accessed | tf_op | source)
XLA Modules:
  0.0 251.5 jit_solution(11523551809146346440)
XLA Ops:
  7.9 5.4 %fusion.4 = bf16[256,1024]{1,0:T(8,128)(2,1)S(1)} fusion(bf16[256,768]{1,0:T(8,128)(2,1)} %param.4, bf16[768,1024]{1,0:T(8,128)(2,1)S(1)} %copy-done, f32[1024]{0:T(1024)} %param.6), kind=kOutput, calls=%fused_computation.23 | convolution fusion | flops 403439616 | bytes 2494464 | tf_op jit(solution)/shard_map/dot_general | solution.py:17
  14.3 2.5 %collective-permute-start = (bf16[256,512]{1,0:T(8,128)(2,1)}, bf16[256,512]{1,0:T(8,128)(2,1)}, u32[]{:S(2)}, u32[]{:S(2)}) collective-permute-start(bf16[256,512]{1,0:T(8,128)(2,1)} %get-tuple-element.9), channel_id=1, source_target_pairs={{0,1},{1,2},{2,3},{3,4},{4,5},{5,6},{6,7},{7,0},{8,9},{9,10},{10,1... | collective-permute-start | bytes 786440 | tf_op jit(solution)/shard_map/ppermute | solution.py:33
  16.8 4.0 %collective-permute-start.4 = (bf16[256,512]{1,0:T(8,128)(2,1)}, bf16[256,512]{1,0:T(8,128)(2,1)S(1)}, u32[]{:S(2)}, u32[]{:S(2)}) collective-permute-start(bf16[256,512]{1,0:T(8,128)(2,1)} %get-tuple-element.9), channel_id=1, source_target_pairs={{0,7},{1,0},{2,1},{3,2},{4,3},{5,4},{6,5},{7,6},{8,15},{9,8},{10,9... | collective-permute-start | bytes 786440 | tf_op jit(solution)/shard_map/ppermute | solution.py:36
  21.6 5.5 %collective-permute-done = bf16[256,512]{1,0:T(8,128)(2,1)} collective-permute-done((bf16[256,512]{1,0:T(8,128)(2,1)}, bf16[256,512]{1,0:T(8,128)(2,1)}, u32[]{:S(2)}, u32[]{:S(2)}) %collective-permute-start) | collective-permute-done | bytes 262176 | tf_op jit(solution)/shard_map/ppermute | solution.py:33
  27.4 9.6 %collective-permute-done.1 = bf16[256,512]{1,0:T(8,128)(2,1)} collective-permute-done((bf16[256,512]{1,0:T(8,128)(2,1)}, bf16[256,512]{1,0:T(8,128)(2,1)}, u32[]{:S(2)}, u32[]{:S(2)}) %collective-permute-start.1) | collective-permute-done | bytes 262176 | tf_op jit(solution)/shard_map/ppermute | solution.py:33
  37.1 2.7 %collective-permute-start.5 = (bf16[256,512]{1,0:T(8,128)(2,1)S(1)}, bf16[256,512]{1,0:T(8,128)(2,1)S(1)}, u32[]{:S(2)}, u32[]{:S(2)}) collective-permute-start(bf16[256,512]{1,0:T(8,128)(2,1)S(1)} %collective-permute-done.4), channel_id=1, source_target_pairs={{0,7},{1,0},{2,1},{3,2},{4,3},{5,4},{6,5},{7,6},{8,15},{9,8},{10,9... | collective-permute-start | bytes 786440 | tf_op jit(solution)/shard_map/ppermute | solution.py:36
  39.8 1.7 bitcast_dynamic-update-slice_fusion.6
  41.5 9.2 %collective-permute-done.2 = bf16[256,512]{1,0:T(8,128)(2,1)S(1)} collective-permute-done((bf16[256,512]{1,0:T(8,128)(2,1)}, bf16[256,512]{1,0:T(8,128)(2,1)S(1)}, u32[]{:S(2)}, u32[]{:S(2)}) %collective-permute-start.2) | collective-permute-done | bytes 262176 | tf_op jit(solution)/shard_map/ppermute | solution.py:33
  50.7 1.7 bitcast_dynamic-update-slice_fusion.5
  52.4 2.7 %collective-permute-start.6 = (bf16[256,512]{1,0:T(8,128)(2,1)S(1)}, bf16[256,512]{1,0:T(8,128)(2,1)S(1)}, u32[]{:S(2)}, u32[]{:S(2)}) collective-permute-start(bf16[256,512]{1,0:T(8,128)(2,1)S(1)} %collective-permute-done.5), channel_id=1, source_target_pairs={{0,7},{1,0},{2,1},{3,2},{4,3},{5,4},{6,5},{7,6},{8,15},{9,8},{10,9... | collective-permute-start | bytes 786440 | tf_op jit(solution)/shard_map/ppermute | solution.py:36
  55.8 8.6 %collective-permute-done.3 = bf16[256,512]{1,0:T(8,128)(2,1)S(1)} collective-permute-done((bf16[256,512]{1,0:T(8,128)(2,1)S(1)}, bf16[256,512]{1,0:T(8,128)(2,1)S(1)}, u32[]{:S(2)}, u32[]{:S(2)}) %collective-permute-start.3) | collective-permute-done | bytes 262176 | tf_op jit(solution)/shard_map/ppermute | solution.py:33
  67.3 3.6 %gather_fusion = bf16[8,256,512]{2,1,0:T(8,128)(2,1)} fusion(bf16[8,256,512]{2,1,0:T(8,128)(2,1)} %bitcast_dynamic-update-slice_fusion, s32[1024]{0:T(1024)S(1)} %pad_clamp_fusion.1), kind=kCustom, calls=%fused_computation | custom fusion | bytes 4194336 | tf_op jit(solution)/shard_map/jit(_take)/gather | solution.py:40
  70.9 2.7 %bitcast_select_fusion = bf16[2048,512]{1,0:T(8,128)(2,1)} fusion(bf16[8,256,512]{2,1,0:T(8,128)(2,1)} %gather_fusion, pred[2048]{0:T(1024)(128)(4,1)S(1)} %broadcast_in_dim.37), kind=kLoop, calls=%fused_computation.10 | loop fusion | flops 1048576 | bytes 4196352 | tf_op jit(solution)/shard_map/jit(_take)/select_n | solution.py:40
  73.6 6.6 %multiply_subtract_fusion = f32[2048,512]{1,0:T(8,128)} fusion(bf16[512,1024]{1,0:T(8,128)(2,1)S(1)} %copy-done.1, f32[512]{0:T(512)S(1)} %multiply_reduce_fusion, bf16[2048,512]{1,0:T(8,128)(2,1)} %bitcast_select_fusion, bf16[2048,512]{1,0:T(8,128)(2,1)} %all-gather.3.cloned.1.call-done), kind=kOutput, calls=%fused_computation.4 | convolution fusion | flops 2157969408 | bytes 9439232 | tf_op jit(solution)/shard_map/dot_general | solution.py:46
  80.3 40.6 %reduce-scatter.2.cloned.1.call-done = f32[256,512]{1,0:T(8,128)} async-done(((f32[2048,512]{1,0:T(8,128)}), f32[256,512]{1,0:T(8,128)}) %reduce-scatter.2.cloned.1.call-update) | async-done | bytes 524304 | tf_op jit(solution)/shard_map/reduce_scatter | solution.py:50
  123.3 5.4 %collective-permute-start.10 = (f32[2,256]{1,0:T(2,128)S(1)}, f32[2,256]{1,0:T(2,128)S(1)}, u32[]{:S(2)}, u32[]{:S(2)}) collective-permute-start(f32[2,256]{1,0:T(2,128)S(1)} %get-tuple-element.10), channel_id=1, source_target_pairs={{0,4},{1,5},{2,6},{3,7},{4,0},{5,1},{6,2},{7,3},{8,12},{9,13},{10,... | collective-permute-start | bytes 6152 | tf_op jit(solution)/shard_map/ppermute | solution.py:57
  128.8 2.9 %collective-permute-start.12 = (f32[2,256]{1,0:T(2,128)S(1)}, f32[2,256]{1,0:T(2,128)S(1)}, u32[]{:S(2)}, u32[]{:S(2)}) collective-permute-start(f32[2,256]{1,0:T(2,128)S(1)} %get-tuple-element.10), channel_id=1, source_target_pairs={{0,6},{1,7},{2,0},{3,1},{4,2},{5,3},{6,4},{7,5},{8,14},{9,15},{10,... | collective-permute-start | bytes 6152 | tf_op jit(solution)/shard_map/ppermute | solution.py:57
  132.4 3.6 %collective-permute-start.9 = (f32[2,256]{1,0:T(2,128)S(1)}, f32[2,256]{1,0:T(2,128)S(1)}, u32[]{:S(2)}, u32[]{:S(2)}) collective-permute-start(f32[2,256]{1,0:T(2,128)S(1)} %get-tuple-element.10), channel_id=1, source_target_pairs={{0,3},{1,4},{2,5},{3,6},{4,7},{5,0},{6,1},{7,2},{8,11},{9,12},{10,... | collective-permute-start | bytes 6152 | tf_op jit(solution)/shard_map/ppermute | solution.py:57
  136.0 2.3 collective-permute-start.13
  139.1 1.9 divide_convert_fusion
  142.9 28.7 %all-gather.5.cloned.1.call-done = bf16[2048,512]{1,0:T(8,128)(2,1)} async-done(((bf16[256,512]{1,0:T(8,128)(2,1)}), bf16[2048,512]{1,0:T(8,128)(2,1)}) %all-gather.5.cloned.1.call-update) | async-done | bytes 2097168 | tf_op jit(solution)/shard_map/all_gather | solution.py:63
  171.6 1.9 convert_reduce_fusion
  173.6 4.6 %fusion = f32[384,1024]{1,0:T(8,128)S(1)} fusion(bf16[2048,512]{1,0:T(8,128)(2,1)} %all-gather.5.cloned.1.call-done, bf16[2048,512]{1,0:T(8,128)(2,1)} %bitcast_select_fusion, bf16[2048,512]{1,0:T(8,128)(2,1)} %all-gather.3.cloned.1.call-done), kind=kOutput, calls=%fused_computation.16 | convolution fusion | flops 1619001344 | bytes 7340032 | tf_op jit(solution)/shard_map/dot_general | solution.py:70
  180.6 2.4 collective-permute-start.15
  184.2 1.8 fusion.5
  186.9 5.2 %collective-permute-done.14 = f32[97,1024]{1,0:T(8,128)} collective-permute-done((f32[97,1024]{1,0:T(8,128)}, f32[97,1024]{1,0:T(8,128)}, u32[]{:S(2)}, u32[]{:S(2)}) %collective-permute-start.14) | collective-permute-done | bytes 397344 | tf_op jit(solution)/shard_map/ppermute | solution.py:92
  192.0 12.0 %collective-permute-done.15 = f32[97,1024]{1,0:T(8,128)} collective-permute-done((f32[97,1024]{1,0:T(8,128)}, f32[97,1024]{1,0:T(8,128)}, u32[]{:S(2)}, u32[]{:S(2)}) %collective-permute-start.15) | collective-permute-done | bytes 397344 | tf_op jit(solution)/shard_map/ppermute | solution.py:92
  206.7 1.8 collective-permute-start.17
  208.4 2.9 %collective-permute-start.18 = (f32[96,1024]{1,0:T(8,128)S(1)}, f32[96,1024]{1,0:T(8,128)S(1)}, u32[]{:S(2)}, u32[]{:S(2)}) collective-permute-start(f32[96,1024]{1,0:T(8,128)S(1)} %fusion.19), channel_id=1, source_target_pairs={{0,128},{64,192},{128,0},{192,64},{1,129},{65,193},{129,1},{193,65... | collective-permute-start | bytes 1179656 | tf_op jit(solution)/shard_map/ppermute | solution.py:99
  211.9 23.1 %all-reduce.4.cloned.1.call-done = f32[129,1024]{1,0:T(8,128)} async-done(((f32[129,1024]{1,0:T(8,128)}), f32[129,1024]{1,0:T(8,128)}) %all-reduce.4.cloned.1.call-update) | async-done | bytes 528400 | tf_op jit(solution)/shard_map/psum | solution.py:82
  235.6 2.1 fusion.6
  240.1 1.8 gather_fusion.1
  (96 shorter events, 26.7 us)
Async XLA Ops:
  6.5 1.4 copy-start
  6.5 20.5 %copy-start.1 = (bf16[512,1024]{1,0:T(8,128)(2,1)S(1)}, bf16[512,1024]{1,0:T(8,128)(2,1)}, u32[]{:S(2)}) copy-start(bf16[512,1024]{1,0:T(8,128)(2,1)} %param.7) | copy-start | bytes 3145732
  6.5 67.1 %all-gather.3.cloned.1.call-start = ((), (), s32[]{:S(2)}) async-start(), calls=%async_computation.1 | async-start | bytes 2359296 | tf_op jit(solution)/shard_map/all_gather | solution.py:26
  14.2 106.7 %reduce-scatter.2.cloned.1.call-start = ((), (), s32[]{:S(2)}) async-start(), calls=%async_computation.2 | async-start | bytes 4718592 | tf_op jit(solution)/shard_map/reduce_scatter | solution.py:50
  14.3 12.8 %collective-permute-start = (bf16[256,512]{1,0:T(8,128)(2,1)}, bf16[256,512]{1,0:T(8,128)(2,1)}, u32[]{:S(2)}, u32[]{:S(2)}) collective-permute-start(bf16[256,512]{1,0:T(8,128)(2,1)} %get-tuple-element.9), channel_id=1, source_target_pairs={{0,1},{1,2},{2,3},{3,4},{4,5},{5,6},{6,7},{7,0},{8,9},{9,10},{10,1... | collective-permute-start | bytes 786440 | tf_op jit(solution)/shard_map/ppermute | solution.py:33
  16.8 20.3 %collective-permute-start.4 = (bf16[256,512]{1,0:T(8,128)(2,1)}, bf16[256,512]{1,0:T(8,128)(2,1)S(1)}, u32[]{:S(2)}, u32[]{:S(2)}) collective-permute-start(bf16[256,512]{1,0:T(8,128)(2,1)} %get-tuple-element.9), channel_id=1, source_target_pairs={{0,7},{1,0},{2,1},{3,2},{4,3},{5,4},{6,5},{7,6},{8,15},{9,8},{10,9... | collective-permute-start | bytes 786440 | tf_op jit(solution)/shard_map/ppermute | solution.py:36
  27.1 9.9 %collective-permute-start.1 = (bf16[256,512]{1,0:T(8,128)(2,1)}, bf16[256,512]{1,0:T(8,128)(2,1)}, u32[]{:S(2)}, u32[]{:S(2)}) collective-permute-start(bf16[256,512]{1,0:T(8,128)(2,1)} %collective-permute-done), channel_id=1, source_target_pairs={{0,1},{1,2},{2,3},{3,4},{4,5},{5,6},{6,7},{7,0},{8,9},{9,10},{10,1... | collective-permute-start | bytes 786440 | tf_op jit(solution)/shard_map/ppermute | solution.py:33
  37.0 13.8 %collective-permute-start.2 = (bf16[256,512]{1,0:T(8,128)(2,1)}, bf16[256,512]{1,0:T(8,128)(2,1)S(1)}, u32[]{:S(2)}, u32[]{:S(2)}) collective-permute-start(bf16[256,512]{1,0:T(8,128)(2,1)} %collective-permute-done.1), channel_id=1, source_target_pairs={{0,1},{1,2},{2,3},{3,4},{4,5},{5,6},{6,7},{7,0},{8,9},{9,10},{10,1... | collective-permute-start | bytes 786440 | tf_op jit(solution)/shard_map/ppermute | solution.py:33
  37.1 15.3 %collective-permute-start.5 = (bf16[256,512]{1,0:T(8,128)(2,1)S(1)}, bf16[256,512]{1,0:T(8,128)(2,1)S(1)}, u32[]{:S(2)}, u32[]{:S(2)}) collective-permute-start(bf16[256,512]{1,0:T(8,128)(2,1)S(1)} %collective-permute-done.4), channel_id=1, source_target_pairs={{0,7},{1,0},{2,1},{3,2},{4,3},{5,4},{6,5},{7,6},{8,15},{9,8},{10,9... | collective-permute-start | bytes 786440 | tf_op jit(solution)/shard_map/ppermute | solution.py:36
  50.7 13.7 %collective-permute-start.3 = (bf16[256,512]{1,0:T(8,128)(2,1)S(1)}, bf16[256,512]{1,0:T(8,128)(2,1)S(1)}, u32[]{:S(2)}, u32[]{:S(2)}) collective-permute-start(bf16[256,512]{1,0:T(8,128)(2,1)S(1)} %collective-permute-done.2), channel_id=1, source_target_pairs={{0,1},{1,2},{2,3},{3,4},{4,5},{5,6},{6,7},{7,0},{8,9},{9,10},{10,1... | collective-permute-start | bytes 786440 | tf_op jit(solution)/shard_map/ppermute | solution.py:33
  52.4 12.7 %collective-permute-start.6 = (bf16[256,512]{1,0:T(8,128)(2,1)S(1)}, bf16[256,512]{1,0:T(8,128)(2,1)S(1)}, u32[]{:S(2)}, u32[]{:S(2)}) collective-permute-start(bf16[256,512]{1,0:T(8,128)(2,1)S(1)} %collective-permute-done.5), channel_id=1, source_target_pairs={{0,7},{1,0},{2,1},{3,2},{4,3},{5,4},{6,5},{7,6},{8,15},{9,8},{10,9... | collective-permute-start | bytes 786440 | tf_op jit(solution)/shard_map/ppermute | solution.py:36
  80.2 91.3 %all-gather.5.cloned.1.call-start = ((), (), s32[]{:S(2)}) async-start(), calls=%async_computation.3 | async-start | bytes 2359296 | tf_op jit(solution)/shard_map/all_gather | solution.py:63
  123.3 9.1 %collective-permute-start.10 = (f32[2,256]{1,0:T(2,128)S(1)}, f32[2,256]{1,0:T(2,128)S(1)}, u32[]{:S(2)}, u32[]{:S(2)}) collective-permute-start(f32[2,256]{1,0:T(2,128)S(1)} %get-tuple-element.10), channel_id=1, source_target_pairs={{0,4},{1,5},{2,6},{3,7},{4,0},{5,1},{6,2},{7,3},{8,12},{9,13},{10,... | collective-permute-start | bytes 6152 | tf_op jit(solution)/shard_map/ppermute | solution.py:57
  128.7 7.2 %collective-permute-start.11 = (f32[2,256]{1,0:T(2,128)S(1)}, f32[2,256]{1,0:T(2,128)S(1)}, u32[]{:S(2)}, u32[]{:S(2)}) collective-permute-start(f32[2,256]{1,0:T(2,128)S(1)} %get-tuple-element.10), channel_id=1, source_target_pairs={{0,5},{1,6},{2,7},{3,0},{4,1},{5,2},{6,3},{7,4},{8,13},{9,14},{10,... | collective-permute-start | bytes 6152 | tf_op jit(solution)/shard_map/ppermute | solution.py:57
  128.8 9.5 %collective-permute-start.12 = (f32[2,256]{1,0:T(2,128)S(1)}, f32[2,256]{1,0:T(2,128)S(1)}, u32[]{:S(2)}, u32[]{:S(2)}) collective-permute-start(f32[2,256]{1,0:T(2,128)S(1)} %get-tuple-element.10), channel_id=1, source_target_pairs={{0,6},{1,7},{2,0},{3,1},{4,2},{5,3},{6,4},{7,5},{8,14},{9,15},{10,... | collective-permute-start | bytes 6152 | tf_op jit(solution)/shard_map/ppermute | solution.py:57
  131.7 6.6 %collective-permute-start.7 = (f32[2,256]{1,0:T(2,128)S(1)}, f32[2,256]{1,0:T(2,128)S(1)}, u32[]{:S(2)}, u32[]{:S(2)}) collective-permute-start(f32[2,256]{1,0:T(2,128)S(1)} %get-tuple-element.10), channel_id=1, source_target_pairs={{0,1},{1,2},{2,3},{3,4},{4,5},{5,6},{6,7},{7,0},{8,9},{9,10},{10,1... | collective-permute-start | bytes 6152 | tf_op jit(solution)/shard_map/ppermute | solution.py:57
  131.7 6.6 %collective-permute-start.8 = (f32[2,256]{1,0:T(2,128)S(1)}, f32[2,256]{1,0:T(2,128)S(1)}, u32[]{:S(2)}, u32[]{:S(2)}) collective-permute-start(f32[2,256]{1,0:T(2,128)S(1)} %get-tuple-element.10), channel_id=1, source_target_pairs={{0,2},{1,3},{2,4},{3,5},{4,6},{5,7},{6,0},{7,1},{8,10},{9,11},{10,... | collective-permute-start | bytes 6152 | tf_op jit(solution)/shard_map/ppermute | solution.py:57
  132.4 5.9 %collective-permute-start.9 = (f32[2,256]{1,0:T(2,128)S(1)}, f32[2,256]{1,0:T(2,128)S(1)}, u32[]{:S(2)}, u32[]{:S(2)}) collective-permute-start(f32[2,256]{1,0:T(2,128)S(1)} %get-tuple-element.10), channel_id=1, source_target_pairs={{0,3},{1,4},{2,5},{3,6},{4,7},{5,0},{6,1},{7,2},{8,11},{9,12},{10,... | collective-permute-start | bytes 6152 | tf_op jit(solution)/shard_map/ppermute | solution.py:57
  136.0 3.0 %collective-permute-start.13 = (f32[2,256]{1,0:T(2,128)S(1)}, f32[2,256]{1,0:T(2,128)S(1)}, u32[]{:S(2)}, u32[]{:S(2)}) collective-permute-start(f32[2,256]{1,0:T(2,128)S(1)} %get-tuple-element.10), channel_id=1, source_target_pairs={{0,7},{1,0},{2,1},{3,2},{4,3},{5,4},{6,5},{7,6},{8,15},{9,8},{10,9... | collective-permute-start | bytes 6152 | tf_op jit(solution)/shard_map/ppermute | solution.py:57
  141.1 93.9 %all-reduce.4.cloned.1.call-start = ((), (), s32[]{:S(2)}) async-start(), calls=%async_computation.4 | async-start | bytes 1114112 | tf_op jit(solution)/shard_map/psum | solution.py:82
  173.6 10.6 %copy-start.7 = (bf16[2048,512]{1,0:T(8,128)(2,1)S(1)}, bf16[2048,512]{1,0:T(8,128)(2,1)}, u32[]{:S(2)}) copy-start(bf16[2048,512]{1,0:T(8,128)(2,1)} %all-gather.3.cloned.1.call-done) | copy-start | bytes 6291460
  178.3 5.9 %copy-start.2 = (bf16[2048,512]{1,0:T(8,128)(2,1)S(1)}, bf16[2048,512]{1,0:T(8,128)(2,1)}, u32[]{:S(2)}) copy-start(bf16[2048,512]{1,0:T(8,128)(2,1)} %bitcast_select_fusion) | copy-start | bytes 6291460
  179.4 12.6 %collective-permute-start.14 = (f32[97,1024]{1,0:T(8,128)}, f32[97,1024]{1,0:T(8,128)}, u32[]{:S(2)}, u32[]{:S(2)}) collective-permute-start(f32[97,1024]{1,0:T(8,128)} %get-tuple-element.5), channel_id=1, source_target_pairs={{0,64},{64,128},{128,192},{192,0},{1,65},{65,129},{129,193},{193,1... | collective-permute-start | bytes 1191944 | tf_op jit(solution)/shard_map/ppermute | solution.py:92
  180.6 23.4 %collective-permute-start.15 = (f32[97,1024]{1,0:T(8,128)}, f32[97,1024]{1,0:T(8,128)}, u32[]{:S(2)}, u32[]{:S(2)}) collective-permute-start(f32[97,1024]{1,0:T(8,128)} %get-tuple-element.6), channel_id=1, source_target_pairs={{0,128},{64,192},{128,0},{192,64},{1,129},{65,193},{129,1},{193,65... | collective-permute-start | bytes 1191944 | tf_op jit(solution)/shard_map/ppermute | solution.py:92
  183.0 21.1 %collective-permute-start.16 = (f32[97,1024]{1,0:T(8,128)}, f32[97,1024]{1,0:T(8,128)}, u32[]{:S(2)}, u32[]{:S(2)}) collective-permute-start(f32[97,1024]{1,0:T(8,128)} %get-tuple-element.7), channel_id=1, source_target_pairs={{0,192},{64,0},{128,64},{192,128},{1,193},{65,1},{129,65},{193,129... | collective-permute-start | bytes 1191944 | tf_op jit(solution)/shard_map/ppermute | solution.py:92
  206.7 31.1 %collective-permute-start.17 = (f32[96,1024]{1,0:T(8,128)S(1)}, f32[96,1024]{1,0:T(8,128)S(1)}, u32[]{:S(2)}, u32[]{:S(2)}) collective-permute-start(f32[96,1024]{1,0:T(8,128)S(1)} %fusion.19), channel_id=1, source_target_pairs={{0,64},{64,128},{128,192},{192,0},{1,65},{65,129},{129,193},{193,1... | collective-permute-start | bytes 1179656 | tf_op jit(solution)/shard_map/ppermute | solution.py:99
  208.4 29.3 %collective-permute-start.18 = (f32[96,1024]{1,0:T(8,128)S(1)}, f32[96,1024]{1,0:T(8,128)S(1)}, u32[]{:S(2)}, u32[]{:S(2)}) collective-permute-start(f32[96,1024]{1,0:T(8,128)S(1)} %fusion.19), channel_id=1, source_target_pairs={{0,128},{64,192},{128,0},{192,64},{1,129},{65,193},{129,1},{193,65... | collective-permute-start | bytes 1179656 | tf_op jit(solution)/shard_map/ppermute | solution.py:99
  211.3 26.4 %collective-permute-start.19 = (f32[96,1024]{1,0:T(8,128)S(1)}, f32[96,1024]{1,0:T(8,128)S(1)}, u32[]{:S(2)}, u32[]{:S(2)}) collective-permute-start(f32[96,1024]{1,0:T(8,128)S(1)} %fusion.19), channel_id=1, source_target_pairs={{0,192},{64,0},{128,64},{192,128},{1,193},{65,1},{129,65},{193,129... | collective-permute-start | bytes 1179656 | tf_op jit(solution)/shard_map/ppermute | solution.py:99
  237.7 0.7 copy-start.4
  237.8 0.9 copy-start.5
  237.8 1.0 copy-start.6
  241.9 1.6 copy-start.3
Sparse Core Ops, SparseCore 0:
  14.3 52.0 all-gather.2
  80.3 40.4 reduce-scatter.1
  141.2 30.3 all-gather.4
  187.0 47.9 all-reduce.3

commit v7 on v5

--- a/solution.py
+++ b/solution.py
@@ -33,14 +33,26 @@
 
     local_top = jnp.max(logits, axis=1)
     local_sum = jnp.sum(jnp.exp(logits - local_top[:, None]), axis=1)
-    pair = jnp.stack([local_top, local_sum])
     n_cent = lax.axis_size("cent")
-    received = [pair]
-    for shift in range(1, n_cent):
-        received.append(lax.ppermute(pair, "cent", [(i, (i + shift) % n_cent) for i in range(n_cent)]))
-    stats = jnp.stack(received)
-    top_score = jnp.max(stats[:, 0], axis=0)
-    total = jnp.sum(stats[:, 1] * jnp.exp(stats[:, 0] - top_score[None, :]), axis=0)
+    top_score, total = local_top, local_sum
+    if n_cent & (n_cent - 1) == 0:
+        bit = 1
+        while bit < n_cent:
+            pair = lax.ppermute(
+                jnp.stack([top_score, total]), "cent", [(i, i ^ bit) for i in range(n_cent)]
+            )
+            merged = jnp.maximum(top_score, pair[0])
+            total = total * jnp.exp(top_score - merged) + pair[1] * jnp.exp(pair[0] - merged)
+            top_score = merged
+            bit *= 2
+    else:
+        pair = jnp.stack([local_top, local_sum])
+        received = [pair]
+        for shift in range(1, n_cent):
+            received.append(lax.ppermute(pair, "cent", [(i, (i + shift) % n_cent) for i in range(n_cent)]))
+        stats = jnp.stack(received)
+        top_score = jnp.max(stats[:, 0], axis=0)
+        total = jnp.sum(stats[:, 1] * jnp.exp(stats[:, 0] - top_score[None, :]), axis=0)
     resp = (jnp.exp(logits - top_score[:, None]) / total[:, None]).astype(jnp.bfloat16)
 
     group_resp = lax.all_gather(resp, "feat", axis=0, tiled=True)

time: 247 us -> 247 us (level)
  starting transfers between devices: 25.2 us -> 19 us
  waiting for transfers between devices: 164 us -> 170 us
    ppermute x7 -> x3, starting transfers between devices: 14.9 us -> 8.91 us  [shards(): lax.ppermute(jnp.stack([top_score, total]), 'cent', [(i, i ^ bit) for i i...]
    all_gather x1, waiting for transfers between devices: 28.5 us -> 31.7 us  [shards(): group_resp = lax.all_gather(resp, 'feat', axis=0, tiled=True)]
    ppermute x7 -> x3, waiting for transfers between devices: 0.65 us -> 3.46 us  [shards(): lax.ppermute(jnp.stack([top_score, total]), 'cent', [(i, i ^ bit) for i i...]
  transfers between devices with their start and end apart: 17 -> 13, of which waited for: 8 -> 10; matrix products, arithmetic and copies ran while one was open for 4% -> 4% of each run, Pallas kernels for 0% -> 0%
where the time goes in v7:
time: 247 us; the launch traced here: 246 us
  waiting for transfers between devices  170 us (69%)
  other arithmetic  19.9 us (8%)
  starting transfers between devices  19 us (8%)
  matrix products  18.7 us (8%)
  between operations  13.3 us (5%)
  local copies, waits for them, and re-layouts  4.46 us (2%)
    all_gather x1, waiting for transfers between devices, shards(): group_features = lax.all_gather(features, 'cent', axis=0, tiled=True)  58.2 us
    reduce_scatter x1, waiting for transfers between devices, shards(): lax.psum_scatter(partial_value, 'feat', scatter_dimension=0, tiled=True)  36.6 us
    all_gather x1, waiting for transfers between devices, shards(): group_resp = lax.all_gather(resp, 'feat', axis=0, tiled=True)  31.7 us
    psum x1, waiting for transfers between devices, shards(): lax.psum(jnp.concatenate([row_contract(group_resp[:, :split]), as_rows(ma...  23.1 us
    ppermute x3, waiting for transfers between devices, shards(): owned = owned + lax.ppermute(outgoing, 'dp', ring)  17.3 us
    ppermute x3, starting transfers between devices, shards(): lax.ppermute(jnp.stack([top_score, total]), 'cent', [(i, i ^ bit) for i i...  8.91 us
    dot_general x1, matrix products, shards(): lax.dot_general(group_features, centroids, (((1,), (1,)), ((), ())), pref...  6.56 us
    dot_general x2, matrix products, row_contract(): lax.dot_general(weights, group_features, (((0,), (0,)), ((), ())), prefer...  6.41 us
  transfers between devices with their start and end apart: 13, of which 10 were waited for; matrix products, arithmetic and copies ran while one was open for 4% of the time, Pallas kernels for 0%

profile of v7, /device:TPU:1, one launch (start us, length us, event | category | flops | bytes accessed | tf_op | source)
XLA Modules:
  0.0 245.8 jit_solution(16720908580949563978)
XLA Ops:
  6.5 1.4 copy-done
  7.9 5.8 %fusion.4 = bf16[256,1024]{1,0:T(8,128)(2,1)} fusion(bf16[256,768]{1,0:T(8,128)(2,1)} %param.4, bf16[768,1024]{1,0:T(8,128)(2,1)S(1)} %copy-done, f32[1024]{0:T(1024)} %param.6), kind=kOutput, calls=%fused_computation.20 | convolution fusion | flops 403439616 | bytes 2494464 | tf_op jit(solution)/shard_map/dot_general | solution.py:17
  14.1 58.2 %all-gather.3.cloned.1.call-done = bf16[2048,1024]{1,0:T(8,128)(2,1)} async-done(((bf16[256,1024]{1,0:T(8,128)(2,1)}), bf16[2048,1024]{1,0:T(8,128)(2,1)}) %all-gather.3.cloned.1.call-update) | async-done | bytes 4194320 | tf_op jit(solution)/shard_map/all_gather | solution.py:23
  72.3 6.6 %multiply_subtract_fusion = f32[2048,512]{1,0:T(8,128)} fusion(bf16[2048,1024]{1,0:T(8,128)(2,1)} %all-gather.3.cloned.1.call-done, bf16[512,1024]{1,0:T(8,128)(2,1)S(1)} %copy-done.2, f32[512]{0:T(512)S(1)} %multiply_reduce_fusion), kind=kOutput, calls=%fused_computation.2 | convolution fusion | flops 2149580800 | bytes 9439232 | tf_op jit(solution)/shard_map/dot_general | solution.py:28
  78.9 36.6 %reduce-scatter.2.cloned.1.call-done = f32[256,512]{1,0:T(8,128)} async-done(((f32[2048,512]{1,0:T(8,128)}), f32[256,512]{1,0:T(8,128)}) %reduce-scatter.2.cloned.1.call-update) | async-done | bytes 524304 | tf_op jit(solution)/shard_map/reduce_scatter | solution.py:32
  115.5 1.2 multiply_reduce_fusion.1
  116.7 1.3 exponential_reduce_fusion
  118.0 1.2 collective-permute-start
  119.2 1.3 collective-permute-done
  120.5 2.2 collective-permute-start.1
  122.7 1.2 collective-permute-done.1
  124.0 5.4 %collective-permute-start.2 = (f32[2,256]{1,0:T(2,128)S(1)}, f32[2,256]{1,0:T(2,128)S(1)}, u32[]{:S(2)}, u32[]{:S(2)}) collective-permute-start(f32[2,256]{1,0:T(2,128)S(1)} %pad_maximum_fusion.5), channel_id=1, source_target_pairs={{0,4},{1,5},{2,6},{3,7},{4,0},{5,1},{6,2},{7,3},{8,12},{9,13},{10,... | collective-permute-start | bytes 6152 | tf_op jit(solution)/shard_map/ppermute | solution.py:41
  130.4 1.9 divide_convert_fusion
  132.4 1.6 convert_element_type.17
  134.2 31.7 %all-gather.5.cloned.1.call-done = bf16[2048,512]{1,0:T(8,128)(2,1)} async-done(((bf16[256,512]{1,0:T(8,128)(2,1)}), bf16[2048,512]{1,0:T(8,128)(2,1)}) %all-gather.5.cloned.1.call-update) | async-done | bytes 2097168 | tf_op jit(solution)/shard_map/all_gather | solution.py:58
  165.9 1.9 convert_reduce_fusion
  167.9 4.6 %fusion = f32[384,1024]{1,0:T(8,128)S(1)} fusion(bf16[2048,1024]{1,0:T(8,128)(2,1)} %all-gather.3.cloned.1.call-done, bf16[2048,512]{1,0:T(8,128)(2,1)} %all-gather.5.cloned.1.call-done), kind=kOutput, calls=%fused_computation.13 | convolution fusion | flops 1610612736 | bytes 7340032 | tf_op jit(solution)/shard_map/dot_general | solution.py:65
  173.7 1.2 collective-permute-start.3
  174.9 2.4 collective-permute-start.4
  177.3 1.2 collective-permute-start.5
  178.5 1.8 fusion.6
  181.2 5.2 %collective-permute-done.3 = f32[97,1024]{1,0:T(8,128)} collective-permute-done((f32[97,1024]{1,0:T(8,128)}, f32[97,1024]{1,0:T(8,128)}, u32[]{:S(2)}, u32[]{:S(2)}) %collective-permute-start.3) | collective-permute-done | bytes 397344 | tf_op jit(solution)/shard_map/ppermute | solution.py:87
  186.3 11.9 %collective-permute-done.4 = f32[97,1024]{1,0:T(8,128)} collective-permute-done((f32[97,1024]{1,0:T(8,128)}, f32[97,1024]{1,0:T(8,128)}, u32[]{:S(2)}, u32[]{:S(2)}) %collective-permute-start.4) | collective-permute-done | bytes 397344 | tf_op jit(solution)/shard_map/ppermute | solution.py:87
  198.4 1.4 fusion.14
  200.9 1.8 collective-permute-start.6
  202.7 3.0 %collective-permute-start.7 = (f32[96,1024]{1,0:T(8,128)S(1)}, f32[96,1024]{1,0:T(8,128)S(1)}, u32[]{:S(2)}, u32[]{:S(2)}) collective-permute-start(f32[96,1024]{1,0:T(8,128)S(1)} %fusion.19), channel_id=1, source_target_pairs={{0,128},{64,192},{128,0},{192,64},{1,129},{65,193},{129,1},{193,65... | collective-permute-start | bytes 1179656 | tf_op jit(solution)/shard_map/ppermute | solution.py:94
  206.2 23.1 %all-reduce.4.cloned.1.call-done = f32[129,1024]{1,0:T(8,128)} async-done(((f32[129,1024]{1,0:T(8,128)}), f32[129,1024]{1,0:T(8,128)}) %all-reduce.4.cloned.1.call-update) | async-done | bytes 528400 | tf_op jit(solution)/shard_map/psum | solution.py:77
  229.9 2.1 fusion.5
  233.0 1.3 pad_maximum_fusion.1
  234.4 1.8 gather_fusion
  236.2 1.6 bitcast_select_fusion
  237.8 1.5 pad_maximum_fusion
  (52 shorter events, 7.3 us)
Async XLA Ops:
  6.5 1.4 copy-start
  6.5 7.2 %copy-start.2 = (bf16[512,1024]{1,0:T(8,128)(2,1)S(1)}, bf16[512,1024]{1,0:T(8,128)(2,1)}, u32[]{:S(2)}) copy-start(bf16[512,1024]{1,0:T(8,128)(2,1)} %param.7) | copy-start | bytes 3145732
  6.5 65.7 %all-gather.3.cloned.1.call-start = ((), (), s32[]{:S(2)}) async-start(), calls=%async_computation.1 | async-start | bytes 4718592 | tf_op jit(solution)/shard_map/all_gather | solution.py:23
  13.7 101.8 %reduce-scatter.2.cloned.1.call-start = ((), (), s32[]{:S(2)}) async-start(), calls=%async_computation.2 | async-start | bytes 4718592 | tf_op jit(solution)/shard_map/reduce_scatter | solution.py:32
  78.8 87.0 %all-gather.5.cloned.1.call-start = ((), (), s32[]{:S(2)}) async-start(), calls=%async_computation.3 | async-start | bytes 2359296 | tf_op jit(solution)/shard_map/all_gather | solution.py:58
  118.0 2.5 %collective-permute-start = (f32[2,256]{1,0:T(2,128)S(1)}, f32[2,256]{1,0:T(2,128)S(1)}, u32[]{:S(2)}, u32[]{:S(2)}) collective-permute-start(f32[2,256]{1,0:T(2,128)S(1)} %pad_maximum_fusion.3), channel_id=1, source_target_pairs={{0,1},{1,0},{2,3},{3,2},{4,5},{5,4},{6,7},{7,6},{8,9},{9,8},{10,11... | collective-permute-start | bytes 6152 | tf_op jit(solution)/shard_map/ppermute | solution.py:41
  120.5 3.4 %collective-permute-start.1 = (f32[2,256]{1,0:T(2,128)S(1)}, f32[2,256]{1,0:T(2,128)S(1)}, u32[]{:S(2)}, u32[]{:S(2)}) collective-permute-start(f32[2,256]{1,0:T(2,128)S(1)} %pad_maximum_fusion.4), channel_id=1, source_target_pairs={{0,2},{1,3},{2,0},{3,1},{4,6},{5,7},{6,4},{7,5},{8,10},{9,11},{10,... | collective-permute-start | bytes 6152 | tf_op jit(solution)/shard_map/ppermute | solution.py:41
  124.0 6.4 %collective-permute-start.2 = (f32[2,256]{1,0:T(2,128)S(1)}, f32[2,256]{1,0:T(2,128)S(1)}, u32[]{:S(2)}, u32[]{:S(2)}) collective-permute-start(f32[2,256]{1,0:T(2,128)S(1)} %pad_maximum_fusion.5), channel_id=1, source_target_pairs={{0,4},{1,5},{2,6},{3,7},{4,0},{5,1},{6,2},{7,3},{8,12},{9,13},{10,... | collective-permute-start | bytes 6152 | tf_op jit(solution)/shard_map/ppermute | solution.py:41
  132.4 96.9 %all-reduce.4.cloned.1.call-start = ((), (), s32[]{:S(2)}) async-start(), calls=%async_computation.4 | async-start | bytes 1114112 | tf_op jit(solution)/shard_map/psum | solution.py:77
  167.9 10.5 %copy-start.1 = (bf16[2048,1024]{1,0:T(8,128)(2,1)S(1)}, bf16[2048,1024]{1,0:T(8,128)(2,1)}, u32[]{:S(2)}) copy-start(bf16[2048,1024]{1,0:T(8,128)(2,1)} %all-gather.3.cloned.1.call-done) | copy-start | bytes 12582916
  173.7 12.6 %collective-permute-start.3 = (f32[97,1024]{1,0:T(8,128)}, f32[97,1024]{1,0:T(8,128)}, u32[]{:S(2)}, u32[]{:S(2)}) collective-permute-start(f32[97,1024]{1,0:T(8,128)} %get-tuple-element.11), channel_id=1, source_target_pairs={{0,64},{64,128},{128,192},{192,0},{1,65},{65,129},{129,193},{193,1... | collective-permute-start | bytes 1191944 | tf_op jit(solution)/shard_map/ppermute | solution.py:87
  174.9 23.4 %collective-permute-start.4 = (f32[97,1024]{1,0:T(8,128)}, f32[97,1024]{1,0:T(8,128)}, u32[]{:S(2)}, u32[]{:S(2)}) collective-permute-start(f32[97,1024]{1,0:T(8,128)} %get-tuple-element.12), channel_id=1, source_target_pairs={{0,128},{64,192},{128,0},{192,64},{1,129},{65,193},{129,1},{193,65... | collective-permute-start | bytes 1191944 | tf_op jit(solution)/shard_map/ppermute | solution.py:87
  177.3 21.1 %collective-permute-start.5 = (f32[97,1024]{1,0:T(8,128)}, f32[97,1024]{1,0:T(8,128)}, u32[]{:S(2)}, u32[]{:S(2)}) collective-permute-start(f32[97,1024]{1,0:T(8,128)} %get-tuple-element.13), channel_id=1, source_target_pairs={{0,192},{64,0},{128,64},{192,128},{1,193},{65,1},{129,65},{193,129... | collective-permute-start | bytes 1191944 | tf_op jit(solution)/shard_map/ppermute | solution.py:87
  200.9 31.1 %collective-permute-start.6 = (f32[96,1024]{1,0:T(8,128)S(1)}, f32[96,1024]{1,0:T(8,128)S(1)}, u32[]{:S(2)}, u32[]{:S(2)}) collective-permute-start(f32[96,1024]{1,0:T(8,128)S(1)} %fusion.19), channel_id=1, source_target_pairs={{0,64},{64,128},{128,192},{192,0},{1,65},{65,129},{129,193},{193,1... | collective-permute-start | bytes 1179656 | tf_op jit(solution)/shard_map/ppermute | solution.py:94
  202.7 29.3 %collective-permute-start.7 = (f32[96,1024]{1,0:T(8,128)S(1)}, f32[96,1024]{1,0:T(8,128)S(1)}, u32[]{:S(2)}, u32[]{:S(2)}) collective-permute-start(f32[96,1024]{1,0:T(8,128)S(1)} %fusion.19), channel_id=1, source_target_pairs={{0,128},{64,192},{128,0},{192,64},{1,129},{65,193},{129,1},{193,65... | collective-permute-start | bytes 1179656 | tf_op jit(solution)/shard_map/ppermute | solution.py:94
  205.7 26.4 %collective-permute-start.8 = (f32[96,1024]{1,0:T(8,128)S(1)}, f32[96,1024]{1,0:T(8,128)S(1)}, u32[]{:S(2)}, u32[]{:S(2)}) collective-permute-start(f32[96,1024]{1,0:T(8,128)S(1)} %fusion.19), channel_id=1, source_target_pairs={{0,192},{64,0},{128,64},{192,128},{1,193},{65,1},{129,65},{193,129... | collective-permute-start | bytes 1179656 | tf_op jit(solution)/shard_map/ppermute | solution.py:94
  232.0 0.8 copy-start.4
  232.0 0.9 copy-start.5
  232.1 1.0 copy-start.6
  236.2 1.6 copy-start.3
Sparse Core Ops, SparseCore 0:
  13.8 58.3 all-gather.2
  79.0 36.5 reduce-scatter.1
  132.5 33.3 all-gather.4
  181.3 47.9 all-reduce.3
